TPU v7x, 32 devices: a whole 2x2x4 slice. The times are simulated.
32 devices in a mesh: dom: 32 (over z, y, x, core).
Axes of the slice: x: 2, y: 2, z: 4, core: 2. Of those that a mesh axis runs over, the one named last changes fastest.
Arguments:
- x_block: float32 [8, 49152], P(None, 'dom'), may hold values from -18 to 18
- p_block: float32 [8, 49152], P(None, 'dom'), may hold values from -18 to 18
- stiff_elem: float32 [20, 20, 8192], P(None, None, 'dom'), may hold values from -6 to 12.4, as said below
- mass_elem: float32 [20, 20, 8192], P(None, None, 'dom'), may hold values from -0.03 to 0.7, as said below
- node_elem: float32 [10, 10, 8192], P(None, None, 'dom'), may hold values from -1 to 6.1, as said below
- elem_edge: int32 [20, 8192], P(None, 'dom'), may hold values from 0 to 1919, as said below
- elem_node: int32 [10, 8192], P(None, 'dom'), may hold values from 0 to 575, as said below
- send_edge: int32 [6, 2048], P(None, 'dom'), may hold values from 0 to 1535, as said below
- send_node: int32 [6, 1024], P(None, 'dom'), may hold values from 0 to 383, as said below
- grad_pairs: int32 [2, 49152], P(None, 'dom'), may hold values from 0 to 575, as said below
Outputs:
- w_block: float32 [8, 49152], P(None, 'dom')
- gram_stiff: float32 [24, 24], replicated
- gram_mass: float32 [24, 24], replicated
Inputs may be any that keep to these rules, and one draw needn't show every extreme that they name: `stiff_elem`: each element's matrix is symmetric and positive definite. `mass_elem`: each element's matrix is symmetric and positive definite. `node_elem`: each element's matrix is symmetric and positive definite. `elem_edge`: the 20 entries of one element are distinct, and every entry of a subdomain's extended edge list is used by some element of that subdomain. `elem_node`: the 10 entries of one element are distinct, and every entry of a subdomain's extended nodal list is used by some element of that subdomain. `send_edge`: the 64 entries of one direction of one subdomain are distinct. `send_node`: the 32 entries of one direction of one subdomain are distinct. `grad_pairs`: the tail and head of one edge unknown differ.
All inputs are finite; a program needn't handle non-finite values.
Results may differ from a plain program's by a relative error of at most 0.0001.
Values sent between devices are 32-bit elements; how exact they have to be, the bound alone decides.
No kernel may reach another device: no remote copies, remote signals or barrier semaphores. Data moves between devices by JAX's collectives and lax.ppermute only.
A program may use at most 128 MiB of HBM per device.

v0:
```python
import jax
import jax.numpy as jnp
from jax import lax
from jax.sharding import PartitionSpec as P

CHEB_DEG = 3
NNODE = 384


highest = lax.Precision.HIGHEST
OFFSETS = (1, -1, 4, -4, 16, -16)
interval_low = 0.3
interval_high = 1.7
jacobi_weight = 0.7


def from_behind(shard, axis, by):
    length = lax.axis_size(axis)
    return lax.ppermute(shard, axis, [(i, (i + by) % length) for i in range(length)])


def edge_extend(values, send_edge):
    pieces = [values]
    for direction in range(6):
        outgoing = values[:, send_edge[direction]]
        pieces.append(from_behind(outgoing, "dom", OFFSETS[direction]))
    return jnp.concatenate(pieces, axis=1)


def edge_return(extended, send_edge):
    ghosts = send_edge.shape[1]
    owned = extended.shape[1] - 6 * ghosts
    total = extended[:, :owned]
    for direction in range(6):
        start = owned + direction * ghosts
        back = from_behind(extended[:, start : start + ghosts], "dom", -OFFSETS[direction])
        total = total.at[:, send_edge[direction]].add(back)
    return total


def node_extend(values, send_node):
    pieces = [values]
    for direction in range(6):
        outgoing = values[:, send_node[direction]]
        pieces.append(from_behind(outgoing, "dom", OFFSETS[direction]))
    return jnp.concatenate(pieces, axis=1)


def node_return(extended, send_node):
    ghosts = send_node.shape[1]
    owned = extended.shape[1] - 6 * ghosts
    total = extended[:, :owned]
    for direction in range(6):
        start = owned + direction * ghosts
        back = from_behind(extended[:, start : start + ghosts], "dom", -OFFSETS[direction])
        total = total.at[:, send_node[direction]].add(back)
    return total


def element_terms(matrices, values):
    return jnp.einsum("jke,cke->cje", matrices, values, precision=highest)


def scatter_local(terms, connect, length):
    return jnp.zeros((terms.shape[0], length), jnp.float32).at[:, connect].add(terms)


def inner_elements(left, right):
    return jnp.einsum("cke,dke->cd", left, right, precision=highest)


def arrange(pair_part, row_part, modes):
    mode_mode = pair_part[:, :modes, :modes]
    mode_prev = pair_part[:, :modes, modes:]
    prev_mode = pair_part[:, modes:, :modes]
    prev_prev = pair_part[:, modes:, modes:]
    new_mode = jnp.swapaxes(row_part[:, :, :modes], 1, 2)
    new_prev = jnp.swapaxes(row_part[:, :, 2 * modes :], 1, 2)
    upper = jnp.concatenate([mode_mode, new_mode, mode_prev], axis=2)
    lower = jnp.concatenate([prev_mode, new_prev, prev_prev], axis=2)
    return jnp.concatenate([upper, row_part, lower], axis=1)


def shards(
    x_block,
    p_block,
    stiff_elem,
    mass_elem,
    node_elem,
    elem_edge,
    elem_node,
    send_edge,
    send_node,
    grad_pairs,
):
    modes = x_block.shape[0]
    owned_edges = x_block.shape[1]
    edge_length = owned_edges + 6 * send_edge.shape[1]
    node_length = NNODE + 6 * send_node.shape[1]
    pair = jnp.concatenate([x_block, p_block], axis=0)
    pair_values = edge_extend(pair, send_edge)[:, elem_edge]
    stiff_pair = element_terms(stiff_elem, pair_values)
    mass_pair = element_terms(mass_elem, pair_values)
    edge_diag = edge_return(
        scatter_local(jnp.einsum("jje->je", stiff_elem)[None], elem_edge, edge_length), send_edge
    )[0]
    node_diag = node_return(
        scatter_local(jnp.einsum("jje->je", node_elem)[None], elem_node, node_length), send_node
    )[0]
    images = edge_return(
        scatter_local(
            jnp.concatenate([stiff_pair[:modes], mass_pair[:modes]], axis=0), elem_edge, edge_length
        ),
        send_edge,
    )
    stiff_x = images[:modes]
    mass_x = images[modes:]
    numerator, denominator = lax.psum(
        (jnp.sum(x_block * stiff_x, axis=1), jnp.sum(x_block * mass_x, axis=1)), "dom"
    )
    quotient = numerator / denominator
    residual = stiff_x - quotient[:, None] * mass_x

    def stiff_image(vectors):
        values = edge_extend(vectors, send_edge)[:, elem_edge]
        return edge_return(
            scatter_local(element_terms(stiff_elem, values), elem_edge, edge_length), send_edge
        )

    center = 0.5 * (interval_high + interval_low)
    spread = 0.5 * (interval_high - interval_low)
    sigma = center / spread
    rho_now = 1.0 / sigma
    step_dir = residual / (center * edge_diag)
    smooth = step_dir
    for turn in range(CHEB_DEG - 1):
        rho_next = 1.0 / (2.0 * sigma - rho_now)
        remain = residual - stiff_image(smooth)
        step_dir = rho_next * rho_now * step_dir + 2.0 * rho_next / spread * remain / edge_diag
        smooth = smooth + step_dir
        rho_now = rho_next
    after = residual - stiff_image(smooth)
    tails = grad_pairs[0]
    heads = grad_pairs[1]
    gathered_res = (
        jnp.zeros((modes, node_length), jnp.float32)
        .at[:, heads]
        .add(after)
        .at[:, tails]
        .add(-after)
    )
    nodal_res = node_return(gathered_res, send_node)
    first = jacobi_weight * nodal_res / node_diag
    first_values = node_extend(first, send_node)[:, elem_node]
    node_image = node_return(
        scatter_local(element_terms(node_elem, first_values), elem_node, node_length), send_node
    )
    second = first + jacobi_weight * (nodal_res - node_image) / node_diag
    second_full = node_extend(second, send_node)
    w_block = smooth + second_full[:, heads] - second_full[:, tails]
    w_values = edge_extend(w_block, send_edge)[:, elem_edge]
    stiff_wterm = element_terms(stiff_elem, w_values)
    mass_wterm = element_terms(mass_elem, w_values)
    basis_values = jnp.concatenate([pair_values[:modes], w_values, pair_values[modes:]], axis=0)
    w_rows = jnp.stack(
        [inner_elements(stiff_wterm, basis_values), inner_elements(mass_wterm, basis_values)]
    )
    stiff_part = inner_elements(pair_values, stiff_pair)
    mass_part = inner_elements(pair_values, mass_pair)
    full_gram = lax.psum(arrange(jnp.stack([stiff_part, mass_part]), w_rows, modes), "dom")
    total_edges = owned_edges * lax.axis_size("dom")
    return (w_block, full_gram[0] / total_edges, full_gram[1] / total_edges)


def solution(mesh):
    in_specs = (
        P(None, "dom"),
        P(None, "dom"),
        P(None, None, "dom"),
        P(None, None, "dom"),
        P(None, None, "dom"),
        P(None, "dom"),
        P(None, "dom"),
        P(None, "dom"),
        P(None, "dom"),
        P(None, "dom"),
    )
    out_specs = (P(None, "dom"), P(), P())
    return jax.shard_map(shards, mesh=mesh, in_specs=in_specs, out_specs=out_specs, check_vma=False)
```

profile of v0, /device:TPU:0, one launch (start us, length us, event | category | flops | bytes accessed | tf_op | source)
XLA Modules:
  0.0 969.3 jit_solution(670418399362538911)
XLA Ops:
  2.6 27.5 %scatter_custom_fusion.7 = f32[1920]{0:T(1024)S(1)} fusion(s32[5120]{0:T(1024)S(1)} %reshape.805, f32[5120]{0:T(1024)S(1)} %reshape.865, f32[]{:T(128)} %constant.12.clone.1), kind=kCustom, calls=%fused_computation.323 | custom fusion | flops 5120 | bytes 7684 | tf_op jit(solution)/shard_map/scatter-add | solution.py:65
  66.7 6.0 collective-permute-done.2
  87.0 18.8 %gather_fusion.6 = f32[5120,16]{1,0:T(8,128)} fusion(f32[16,1920]{0,1:T(8,128)} %constant_dynamic-update-slice_fusion, s32[5120]{0:T(1024)S(1)} %broadcast_clamp_fusion), kind=kCustom, calls=%fused_computation.6 | custom fusion | bytes 675840 | tf_op jit(solution)/shard_map/gather | solution.py:101
  109.8 6.6 convolution_bitcast_fusion.1
  121.1 6.9 convolution_bitcast_fusion
  136.0 29.1 %scatter_custom_fusion = f32[16,1920]{0,1:T(8,128)} fusion(s32[5120]{0:T(1024)} %copy-done.9, f32[5120,16]{1,0:T(8,128)} %bitcast.321, f32[]{:T(128)} %constant.12.clone.1), kind=kCustom, calls=%fused_computation.143 | custom fusion | flops 81920 | bytes 123392 | tf_op jit(solution)/shard_map/scatter-add | solution.py:65
  184.2 18.2 %scatter_custom_fusion.43 = f32[576]{0:T(1024)S(1)} fusion(s32[2560]{0:T(1024)S(1)} %reshape.1165, f32[2560]{0:T(1024)S(1)} %reshape.1167, f32[]{:T(128)} %constant.12.clone.1), kind=kCustom, calls=%fused_computation.337 | custom fusion | flops 2560 | bytes 2308 | tf_op jit(solution)/shard_map/scatter-add | solution.py:65
  230.9 38.2 %all-reduce = (f32[8]{0:T(128)S(1)}, f32[8]{0:T(128)S(1)}) all-reduce(f32[8]{0:T(128)S(1)} %get-tuple-element.16, f32[8]{0:T(128)S(1)} %get-tuple-element.15), channel_id=1, replica_groups=mesh['dom'=32] {'dom'}, use_global_device_ids=true, to_apply=%region_8.0 | all-reduce | flops 16 | bytes 128 | tf_op jit(solution)/shard_map/psum | solution.py:118
  304.7 18.8 %gather_fusion.13 = f32[5120,8]{1,0:T(8,128)} fusion(f32[8,1920]{0,1:T(8,128)} %constant_dynamic-update-slice_fusion.7, s32[5120]{0:T(1024)S(1)} %broadcast_clamp_fusion), kind=kCustom, calls=%fused_computation.13 | custom fusion | bytes 348160 | tf_op jit(solution)/shard_map/gather | solution.py:125
  327.3 7.2 convolution_bitcast_fusion.7
  338.3 29.1 %scatter_custom_fusion.14 = f32[8,1920]{0,1:T(8,128)} fusion(s32[5120]{0:T(1024)} %copy-done.9, f32[5120,8]{1,0:T(8,128)} %copy.196, f32[]{:T(128)} %constant.12.clone.1), kind=kCustom, calls=%fused_computation.140 | custom fusion | flops 40960 | bytes 61952 | tf_op jit(solution)/shard_map/scatter-add | solution.py:65
  430.6 18.8 %gather_fusion.20 = f32[5120,8]{1,0:T(8,128)} fusion(f32[8,1920]{0,1:T(8,128)} %constant_dynamic-update-slice_fusion.14, s32[5120]{0:T(1024)S(1)} %broadcast_clamp_fusion), kind=kCustom, calls=%fused_computation.20 | custom fusion | bytes 348160 | tf_op jit(solution)/shard_map/gather | solution.py:125
  453.2 7.2 convolution_bitcast_fusion.6
  464.3 29.1 %scatter_custom_fusion.21 = f32[8,1920]{0,1:T(8,128)} fusion(s32[5120]{0:T(1024)} %copy-done.9, f32[5120,8]{1,0:T(8,128)} %copy.200, f32[]{:T(128)} %constant.12.clone.1), kind=kCustom, calls=%fused_computation.138 | custom fusion | flops 40960 | bytes 61952 | tf_op jit(solution)/shard_map/scatter-add | solution.py:65
  556.0 18.8 %gather_fusion.27 = f32[5120,8]{1,0:T(8,128)} fusion(f32[8,1920]{0,1:T(8,128)} %constant_dynamic-update-slice_fusion.21, s32[5120]{0:T(1024)S(1)} %broadcast_clamp_fusion), kind=kCustom, calls=%fused_computation.27 | custom fusion | bytes 348160 | tf_op jit(solution)/shard_map/gather | solution.py:125
  578.6 7.2 convolution_bitcast_fusion.5
  589.7 29.1 %scatter_custom_fusion.28 = f32[8,1920]{0,1:T(8,128)} fusion(s32[5120]{0:T(1024)} %copy-done.9, f32[5120,8]{1,0:T(8,128)} %copy.204, f32[]{:T(128)} %constant.12.clone.1), kind=kCustom, calls=%fused_computation.136 | custom fusion | flops 40960 | bytes 61952 | tf_op jit(solution)/shard_map/scatter-add | solution.py:65
  660.2 9.4 scatter_custom_fusion.35
  669.6 9.4 scatter_custom_fusion.36
  755.3 6.3 convolution_bitcast_fusion.4
  766.1 15.2 %scatter_custom_fusion.50 = f32[8,576]{0,1:T(8,128)} fusion(s32[2560]{0:T(1024)S(1)} %reshape.1165, f32[2560,8]{1,0:T(8,128)} %copy.208, f32[]{:T(128)} %constant.12.clone.1), kind=kCustom, calls=%fused_computation.152 | custom fusion | flops 20480 | bytes 18944 | tf_op jit(solution)/shard_map/scatter-add | solution.py:65
  887.2 18.8 %gather_fusion.49 = f32[5120,8]{1,0:T(8,128)} fusion(f32[8,1920]{0,1:T(8,128)} %constant_dynamic-update-slice_fusion.42, s32[5120]{0:T(1024)S(1)} %broadcast_clamp_fusion), kind=kCustom, calls=%fused_computation.49 | custom fusion | bytes 348160 | tf_op jit(solution)/shard_map/gather | solution.py:161
  909.9 8.3 convolution_bitcast_fusion.2
  929.6 38.8 %psum.23 = f32[2,24,24]{2,1,0:T(8,128)S(1)} all-reduce(f32[2,24,24]{2,1,0:T(8,128)S(1)} %fusion.71), channel_id=1, replica_groups=mesh['dom'=32] {'dom'}, use_global_device_ids=true, to_apply=%region_63.0 | all-reduce | flops 1152 | bytes 9216 | tf_op jit(solution)/shard_map/psum | solution.py:170
  (487 shorter events, 544.6 us)
Async XLA Ops:
  30.7 137.8 %collective-permute-start.17 = (f32[1,64]{1,0:T(1,128)}, f32[1,64]{1,0:T(1,128)}, u32[]{:S(2)}, u32[]{:S(2)}) collective-permute-start(f32[1,64]{1,0:T(1,128)} %get-tuple-element.78), channel_id=1, source_target_pairs={{0,16},{1,17},{2,18},{3,19},{4,20},{5,21},{6,22},{7,23},{8,24},{9,... | collective-permute-start | bytes 776 | tf_op jit(solution)/shard_map/ppermute | solution.py:19
  34.8 133.8 %collective-permute-start.16 = (f32[1,64]{1,0:T(1,128)}, f32[1,64]{1,0:T(1,128)}, u32[]{:S(2)}, u32[]{:S(2)}) collective-permute-start(f32[1,64]{1,0:T(1,128)} %get-tuple-element.79), channel_id=1, source_target_pairs={{0,16},{1,17},{2,18},{3,19},{4,20},{5,21},{6,22},{7,23},{8,24},{9,... | collective-permute-start | bytes 776 | tf_op jit(solution)/shard_map/ppermute | solution.py:19
  34.8 139.1 %collective-permute-start.15 = (f32[1,64]{1,0:T(1,128)}, f32[1,64]{1,0:T(1,128)}, u32[]{:S(2)}, u32[]{:S(2)}) collective-permute-start(f32[1,64]{1,0:T(1,128)} %get-tuple-element.80), channel_id=1, source_target_pairs={{0,4},{1,5},{2,6},{3,7},{4,8},{5,9},{6,10},{7,11},{8,12},{9,13},{1... | collective-permute-start | bytes 776 | tf_op jit(solution)/shard_map/ppermute | solution.py:19
  36.6 137.3 %collective-permute-start.14 = (f32[1,64]{1,0:T(1,128)}, f32[1,64]{1,0:T(1,128)}, u32[]{:S(2)}, u32[]{:S(2)}) collective-permute-start(f32[1,64]{1,0:T(1,128)} %get-tuple-element.81), channel_id=1, source_target_pairs={{0,28},{1,29},{2,30},{3,31},{4,0},{5,1},{6,2},{7,3},{8,4},{9,5},{1... | collective-permute-start | bytes 776 | tf_op jit(solution)/shard_map/ppermute | solution.py:19
  173.9 52.2 %collective-permute-start.11 = (f32[16,64]{0,1:T(8,128)S(1)}, f32[16,64]{0,1:T(8,128)S(1)}, u32[]{:S(2)}, u32[]{:S(2)}) collective-permute-start(f32[16,64]{0,1:T(8,128)S(1)} %get-tuple-element.49), channel_id=1, source_target_pairs={{0,16},{1,17},{2,18},{3,19},{4,20},{5,21},{6,22},{7,23},{8,24},{9,... | collective-permute-start | bytes 12296 | tf_op jit(solution)/shard_map/ppermute | solution.py:19
  173.9 49.2 %collective-permute-start.10 = (f32[16,64]{0,1:T(8,128)S(1)}, f32[16,64]{0,1:T(8,128)S(1)}, u32[]{:S(2)}, u32[]{:S(2)}) collective-permute-start(f32[16,64]{0,1:T(8,128)S(1)} %get-tuple-element.50), channel_id=1, source_target_pairs={{0,16},{1,17},{2,18},{3,19},{4,20},{5,21},{6,22},{7,23},{8,24},{9,... | collective-permute-start | bytes 12296 | tf_op jit(solution)/shard_map/ppermute | solution.py:19
  177.4 42.7 %collective-permute-start.9 = (f32[16,64]{0,1:T(8,128)S(1)}, f32[16,64]{0,1:T(8,128)S(1)}, u32[]{:S(2)}, u32[]{:S(2)}) collective-permute-start(f32[16,64]{0,1:T(8,128)S(1)} %get-tuple-element.51), channel_id=1, source_target_pairs={{0,4},{1,5},{2,6},{3,7},{4,8},{5,9},{6,10},{7,11},{8,12},{9,13},{1... | collective-permute-start | bytes 12296 | tf_op jit(solution)/shard_map/ppermute | solution.py:19
  177.4 39.6 %collective-permute-start.8 = (f32[16,64]{0,1:T(8,128)S(1)}, f32[16,64]{0,1:T(8,128)}, u32[]{:S(2)}, u32[]{:S(2)}) collective-permute-start(f32[16,64]{0,1:T(8,128)S(1)} %get-tuple-element.52), channel_id=1, source_target_pairs={{0,28},{1,29},{2,30},{3,31},{4,0},{5,1},{6,2},{7,3},{8,4},{9,5},{1... | collective-permute-start | bytes 12296 | tf_op jit(solution)/shard_map/ppermute | solution.py:19
  182.1 31.8 %collective-permute-start.7 = (f32[16,64]{0,1:T(8,128)S(1)}, f32[16,64]{0,1:T(8,128)}, u32[]{:S(2)}, u32[]{:S(2)}) collective-permute-start(f32[16,64]{0,1:T(8,128)S(1)} %get-tuple-element.53), channel_id=1, source_target_pairs={{0,1},{1,2},{2,3},{3,4},{4,5},{5,6},{6,7},{7,8},{8,9},{9,10},{10,1... | collective-permute-start | bytes 12296 | tf_op jit(solution)/shard_map/ppermute | solution.py:19
  281.4 22.6 %collective-permute-start.23 = (f32[8,64]{0,1:T(8,128)S(1)}, f32[8,64]{0,1:T(8,128)S(1)}, u32[]{:S(2)}, u32[]{:S(2)}) collective-permute-start(f32[8,64]{0,1:T(8,128)S(1)} %bitcast.348), channel_id=1, source_target_pairs={{0,16},{1,17},{2,18},{3,19},{4,20},{5,21},{6,22},{7,23},{8,24},{9,... | collective-permute-start | bytes 6152 | tf_op jit(solution)/shard_map/ppermute | solution.py:19
  369.0 26.9 %collective-permute-start.29 = (f32[8,64]{0,1:T(8,128)S(1)}, f32[8,64]{0,1:T(8,128)S(1)}, u32[]{:S(2)}, u32[]{:S(2)}) collective-permute-start(f32[8,64]{0,1:T(8,128)S(1)} %get-tuple-element.43), channel_id=1, source_target_pairs={{0,16},{1,17},{2,18},{3,19},{4,20},{5,21},{6,22},{7,23},{8,24},{9,... | collective-permute-start | bytes 6152 | tf_op jit(solution)/shard_map/ppermute | solution.py:19
  369.3 23.5 %collective-permute-start.28 = (f32[8,64]{0,1:T(8,128)S(1)}, f32[8,64]{0,1:T(8,128)S(1)}, u32[]{:S(2)}, u32[]{:S(2)}) collective-permute-start(f32[8,64]{0,1:T(8,128)S(1)} %get-tuple-element.44), channel_id=1, source_target_pairs={{0,16},{1,17},{2,18},{3,19},{4,20},{5,21},{6,22},{7,23},{8,24},{9,... | collective-permute-start | bytes 6152 | tf_op jit(solution)/shard_map/ppermute | solution.py:19
  494.3 26.9 %collective-permute-start.41 = (f32[8,64]{0,1:T(8,128)S(1)}, f32[8,64]{0,1:T(8,128)S(1)}, u32[]{:S(2)}, u32[]{:S(2)}) collective-permute-start(f32[8,64]{0,1:T(8,128)S(1)} %get-tuple-element.37), channel_id=1, source_target_pairs={{0,16},{1,17},{2,18},{3,19},{4,20},{5,21},{6,22},{7,23},{8,24},{9,... | collective-permute-start | bytes 6152 | tf_op jit(solution)/shard_map/ppermute | solution.py:19
  620.9 36.0 %collective-permute-start.53 = (f32[8,64]{0,1:T(8,128)S(1)}, f32[8,64]{0,1:T(8,128)S(1)}, u32[]{:S(2)}, u32[]{:S(2)}) collective-permute-start(f32[8,64]{0,1:T(8,128)S(1)} %get-tuple-element.31), channel_id=1, source_target_pairs={{0,16},{1,17},{2,18},{3,19},{4,20},{5,21},{6,22},{7,23},{8,24},{9,... | collective-permute-start | bytes 6152 | tf_op jit(solution)/shard_map/ppermute | solution.py:19
  622.6 26.4 %collective-permute-start.52 = (f32[8,64]{0,1:T(8,128)S(1)}, f32[8,64]{0,1:T(8,128)S(1)}, u32[]{:S(2)}, u32[]{:S(2)}) collective-permute-start(f32[8,64]{0,1:T(8,128)S(1)} %get-tuple-element.32), channel_id=1, source_target_pairs={{0,16},{1,17},{2,18},{3,19},{4,20},{5,21},{6,22},{7,23},{8,24},{9,... | collective-permute-start | bytes 6152 | tf_op jit(solution)/shard_map/ppermute | solution.py:19
  623.8 22.1 %collective-permute-start.51 = (f32[8,64]{0,1:T(8,128)S(1)}, f32[8,64]{0,1:T(8,128)}, u32[]{:S(2)}, u32[]{:S(2)}) collective-permute-start(f32[8,64]{0,1:T(8,128)S(1)} %get-tuple-element.33), channel_id=1, source_target_pairs={{0,4},{1,5},{2,6},{3,7},{4,8},{5,9},{6,10},{7,11},{8,12},{9,13},{1... | collective-permute-start | bytes 6152 | tf_op jit(solution)/shard_map/ppermute | solution.py:19
  636.8 45.5 %collective-permute-start.65 = (f32[1,32]{1,0:T(1,128)}, f32[1,32]{1,0:T(1,128)}, u32[]{:S(2)}, u32[]{:S(2)}) collective-permute-start(f32[1,32]{1,0:T(1,128)} %get-tuple-element.96), channel_id=1, source_target_pairs={{0,16},{1,17},{2,18},{3,19},{4,20},{5,21},{6,22},{7,23},{8,24},{9,... | collective-permute-start | bytes 392 | tf_op jit(solution)/shard_map/ppermute | solution.py:19
  639.9 42.7 %collective-permute-start.64 = (f32[1,32]{1,0:T(1,128)}, f32[1,32]{1,0:T(1,128)}, u32[]{:S(2)}, u32[]{:S(2)}) collective-permute-start(f32[1,32]{1,0:T(1,128)} %get-tuple-element.97), channel_id=1, source_target_pairs={{0,16},{1,17},{2,18},{3,19},{4,20},{5,21},{6,22},{7,23},{8,24},{9,... | collective-permute-start | bytes 392 | tf_op jit(solution)/shard_map/ppermute | solution.py:19
  645.9 36.6 %collective-permute-start.63 = (f32[1,32]{1,0:T(1,128)}, f32[1,32]{1,0:T(1,128)}, u32[]{:S(2)}, u32[]{:S(2)}) collective-permute-start(f32[1,32]{1,0:T(1,128)} %get-tuple-element.98), channel_id=1, source_target_pairs={{0,4},{1,5},{2,6},{3,7},{4,8},{5,9},{6,10},{7,11},{8,12},{9,13},{1... | collective-permute-start | bytes 392 | tf_op jit(solution)/shard_map/ppermute | solution.py:19
  649.1 30.6 %collective-permute-start.60 = (f32[1,32]{1,0:T(1,128)}, f32[1,32]{1,0:T(1,128)}, u32[]{:S(2)}, u32[]{:S(2)}) collective-permute-start(f32[1,32]{1,0:T(1,128)} %get-tuple-element.101), channel_id=1, source_target_pairs={{0,31},{1,0},{2,1},{3,2},{4,3},{5,4},{6,5},{7,6},{8,7},{9,8},{10,9... | collective-permute-start | bytes 392 | tf_op jit(solution)/shard_map/ppermute | solution.py:19
  682.6 25.4 %collective-permute-start.58 = (f32[8,32]{0,1:T(8,128)S(1)}, f32[8,32]{0,1:T(8,128)}, u32[]{:S(2)}, u32[]{:S(2)}) collective-permute-start(f32[8,32]{0,1:T(8,128)S(1)} %get-tuple-element.64), channel_id=1, source_target_pairs={{0,16},{1,17},{2,18},{3,19},{4,20},{5,21},{6,22},{7,23},{8,24},{9,... | collective-permute-start | bytes 3080 | tf_op jit(solution)/shard_map/ppermute | solution.py:19
  717.0 23.9 %collective-permute-start.66 = (f32[8,32]{0,1:T(8,128)}, f32[8,32]{0,1:T(8,128)S(1)}, u32[]{:S(2)}, u32[]{:S(2)}) collective-permute-start(f32[8,32]{0,1:T(8,128)} %bitcast.114), channel_id=1, source_target_pairs={{0,1},{1,2},{2,3},{3,4},{4,5},{5,6},{6,7},{7,8},{8,9},{9,10},{10,1... | collective-permute-start | bytes 3080 | tf_op jit(solution)/shard_map/ppermute | solution.py:19
  787.6 24.6 %collective-permute-start.77 = (f32[8,32]{0,1:T(8,128)S(1)}, f32[8,32]{0,1:T(8,128)}, u32[]{:S(2)}, u32[]{:S(2)}) collective-permute-start(f32[8,32]{0,1:T(8,128)S(1)} %get-tuple-element.57), channel_id=1, source_target_pairs={{0,16},{1,17},{2,18},{3,19},{4,20},{5,21},{6,22},{7,23},{8,24},{9,... | collective-permute-start | bytes 3080 | tf_op jit(solution)/shard_map/ppermute | solution.py:19
  858.4 22.3 %collective-permute-start.84 = (f32[8,64]{0,1:T(8,128)S(1)}, f32[8,64]{0,1:T(8,128)S(1)}, u32[]{:S(2)}, u32[]{:S(2)}) collective-permute-start(f32[8,64]{0,1:T(8,128)S(1)} %bitcast.361), channel_id=1, source_target_pairs={{0,1},{1,2},{2,3},{3,4},{4,5},{5,6},{6,7},{7,8},{8,9},{9,10},{10,1... | collective-permute-start | bytes 6152 | tf_op jit(solution)/shard_map/ppermute | solution.py:19
  (105 other events, 2031.5 us)
where the time goes:
time: 980 us; the launch traced here: 969 us
  other arithmetic  342 us (35%)
  local copies, waits for them, and re-layouts  306 us (31%)
  starting transfers between devices  153 us (16%)
  blocking collectives  77 us (8%)
  matrix products  60.7 us (6%)
  waiting for transfers between devices  29.2 us (3%)
    scatter-add x7, other arithmetic, scatter_local(): jnp.zeros((terms.shape[0], length), jnp.float32).at[:, connect].add(terms)  177 us
    ppermute x90, starting transfers between devices, from_behind(): lax.ppermute(shard, axis, [(i, (i + by) % length) for i in range(length)])  153 us
    scatter-add x30, other arithmetic, edge_return(): total = total.at[:, send_edge[direction]].add(back)  79.2 us
    gather x6, local copies, waits for them, and re-layouts, stiff_image(): values = edge_extend(vectors, send_edge)[:, elem_edge]  68 us
    gather x30, local copies, waits for them, and re-layouts, edge_extend(): outgoing = values[:, send_edge[direction]]  55.7 us
    dot_general x8, matrix products, element_terms(): return jnp.einsum('jke,cke->cje', matrices, values, precision=highest)  55.7 us
    psum x1, blocking collectives, shards(): lax.psum(arrange(jnp.stack([stiff_part, mass_part]), w_rows, modes), 'dom')  38.8 us
    psum x1, blocking collectives, shards(): lax.psum((jnp.sum(x_block * stiff_x, axis=1), jnp.sum(x_block * mass_x, a...  38.2 us
  transfers between devices with their start and end apart: 90, of which 13 were waited for; matrix products, arithmetic and copies ran while one was open for 35% of the time, Pallas kernels for 0%

commit v1 on v0

v1 whole, which is shorter than its diff:
```python
import jax
import jax.numpy as jnp
from jax import lax
from jax.sharding import PartitionSpec as P

CHEB_DEG = 3
NNODE = 384
LANES = 128


highest = lax.Precision.HIGHEST
OFFSETS = (1, -1, 4, -4, 16, -16)
interval_low = 0.3
interval_high = 1.7
jacobi_weight = 0.7


def from_behind(shard, axis, by):
    length = lax.axis_size(axis)
    return lax.ppermute(shard, axis, [(i, (i + by) % length) for i in range(length)])


def index_table(index, length):
    groups = -(-length // LANES)
    lo = index % LANES
    hi = index // LANES
    lo_hot = (lo[:, None] == jnp.arange(LANES, dtype=jnp.int32)[None, :]).astype(jnp.float32)
    hi_mask = (hi[None, :] == jnp.arange(groups, dtype=jnp.int32)[:, None]).astype(jnp.float32)
    return lo_hot, hi_mask, length


def gather_cols(values, table):
    lo_hot, hi_mask, length = table
    groups = hi_mask.shape[0]
    rows = values.shape[0]
    padded = jnp.pad(values, ((0, 0), (0, groups * LANES - length)))
    split = padded.reshape(rows, groups, LANES)
    picked = jnp.einsum("rab,nb->ran", split, lo_hot, precision=highest)
    return jnp.sum(picked * hi_mask[None], axis=1)


def scatter_cols(terms, table):
    lo_hot, hi_mask, length = table
    groups = hi_mask.shape[0]
    rows = terms.shape[0]
    spread = terms[:, None, :] * hi_mask[None]
    summed = jnp.einsum("ran,nb->rab", spread, lo_hot, precision=highest)
    return summed.reshape(rows, groups * LANES)[:, :length]


def extend(values, send_table):
    outgoing = gather_cols(values, send_table)
    ghosts = outgoing.shape[1] // 6
    pieces = [values]
    for direction in range(6):
        piece = outgoing[:, direction * ghosts : (direction + 1) * ghosts]
        pieces.append(from_behind(piece, "dom", OFFSETS[direction]))
    return jnp.concatenate(pieces, axis=1)


def give_back(extended, send_table):
    owned = send_table[2]
    ghosts = (extended.shape[1] - owned) // 6
    backs = []
    for direction in range(6):
        start = owned + direction * ghosts
        backs.append(from_behind(extended[:, start : start + ghosts], "dom", -OFFSETS[direction]))
    return extended[:, :owned] + scatter_cols(jnp.concatenate(backs, axis=1), send_table)


def element_terms(matrices, values):
    return jnp.sum(matrices[None, :, :, :] * values[:, None, :, :], axis=2)


def inner_elements(left, right):
    return jnp.einsum("cke,dke->cd", left, right, precision=highest)


def arrange(pair_part, row_part, modes):
    mode_mode = pair_part[:, :modes, :modes]
    mode_prev = pair_part[:, :modes, modes:]
    prev_mode = pair_part[:, modes:, :modes]
    prev_prev = pair_part[:, modes:, modes:]
    new_mode = jnp.swapaxes(row_part[:, :, :modes], 1, 2)
    new_prev = jnp.swapaxes(row_part[:, :, 2 * modes :], 1, 2)
    upper = jnp.concatenate([mode_mode, new_mode, mode_prev], axis=2)
    lower = jnp.concatenate([prev_mode, new_prev, prev_prev], axis=2)
    return jnp.concatenate([upper, row_part, lower], axis=1)


def shards(
    x_block,
    p_block,
    stiff_elem,
    mass_elem,
    node_elem,
    elem_edge,
    elem_node,
    send_edge,
    send_node,
    grad_pairs,
):
    modes = x_block.shape[0]
    owned_edges = x_block.shape[1]
    edofs, elements = elem_edge.shape
    ndofs = elem_node.shape[0]
    edge_length = owned_edges + 6 * send_edge.shape[1]
    node_length = NNODE + 6 * send_node.shape[1]

    edge_table = index_table(elem_edge.reshape(-1), edge_length)
    node_table = index_table(elem_node.reshape(-1), node_length)
    send_edge_table = index_table(send_edge.reshape(-1), owned_edges)
    send_node_table = index_table(send_node.reshape(-1), NNODE)
    tails = grad_pairs[0]
    heads = grad_pairs[1]
    grad_table = index_table(jnp.concatenate([heads, tails]), node_length)

    def edge_values(extended):
        return gather_cols(extended, edge_table).reshape(extended.shape[0], edofs, elements)

    def edge_sum(terms):
        return scatter_cols(terms.reshape(terms.shape[0], -1), edge_table)

    pair = jnp.concatenate([x_block, p_block], axis=0)
    pair_values = edge_values(extend(pair, send_edge_table))
    stiff_pair = element_terms(stiff_elem, pair_values)
    mass_pair = element_terms(mass_elem, pair_values)
    edge_diag_terms = jnp.einsum("jje->je", stiff_elem)[None]
    images = give_back(
        edge_sum(jnp.concatenate([stiff_pair[:modes], mass_pair[:modes], edge_diag_terms], axis=0)),
        send_edge_table,
    )
    stiff_x = images[:modes]
    mass_x = images[modes : 2 * modes]
    edge_diag = images[2 * modes]
    node_diag_terms = jnp.einsum("jje->je", node_elem).reshape(1, -1)
    node_diag = give_back(scatter_cols(node_diag_terms, node_table), send_node_table)[0]
    numerator, denominator = lax.psum(
        (jnp.sum(x_block * stiff_x, axis=1), jnp.sum(x_block * mass_x, axis=1)), "dom"
    )
    quotient = numerator / denominator
    residual = stiff_x - quotient[:, None] * mass_x

    def stiff_image(vectors):
        values = edge_values(extend(vectors, send_edge_table))
        return give_back(edge_sum(element_terms(stiff_elem, values)), send_edge_table)

    center = 0.5 * (interval_high + interval_low)
    spread = 0.5 * (interval_high - interval_low)
    sigma = center / spread
    rho_now = 1.0 / sigma
    step_dir = residual / (center * edge_diag)
    smooth = step_dir
    for turn in range(CHEB_DEG - 1):
        rho_next = 1.0 / (2.0 * sigma - rho_now)
        remain = residual - stiff_image(smooth)
        step_dir = rho_next * rho_now * step_dir + 2.0 * rho_next / spread * remain / edge_diag
        smooth = smooth + step_dir
        rho_now = rho_next
    after = residual - stiff_image(smooth)
    gathered_res = scatter_cols(jnp.concatenate([after, -after], axis=1), grad_table)
    nodal_res = give_back(gathered_res, send_node_table)
    first = jacobi_weight * nodal_res / node_diag
    first_values = gather_cols(extend(first, send_node_table), node_table).reshape(modes, ndofs, elements)
    node_image = give_back(
        scatter_cols(element_terms(node_elem, first_values).reshape(modes, -1), node_table),
        send_node_table,
    )
    second = first + jacobi_weight * (nodal_res - node_image) / node_diag
    ends = gather_cols(extend(second, send_node_table), grad_table)
    w_block = smooth + ends[:, :owned_edges] - ends[:, owned_edges:]
    w_values = edge_values(extend(w_block, send_edge_table))
    stiff_wterm = element_terms(stiff_elem, w_values)
    mass_wterm = element_terms(mass_elem, w_values)
    basis_values = jnp.concatenate([pair_values[:modes], w_values, pair_values[modes:]], axis=0)
    w_rows = jnp.stack(
        [inner_elements(stiff_wterm, basis_values), inner_elements(mass_wterm, basis_values)]
    )
    stiff_part = inner_elements(pair_values, stiff_pair)
    mass_part = inner_elements(pair_values, mass_pair)
    full_gram = lax.psum(arrange(jnp.stack([stiff_part, mass_part]), w_rows, modes), "dom")
    total_edges = owned_edges * lax.axis_size("dom")
    return (w_block, full_gram[0] / total_edges, full_gram[1] / total_edges)


def solution(mesh):
    in_specs = (
        P(None, "dom"),
        P(None, "dom"),
        P(None, None, "dom"),
        P(None, None, "dom"),
        P(None, None, "dom"),
        P(None, "dom"),
        P(None, "dom"),
        P(None, "dom"),
        P(None, "dom"),
        P(None, "dom"),
    )
    out_specs = (P(None, "dom"), P(), P())
    return jax.shard_map(shards, mesh=mesh, in_specs=in_specs, out_specs=out_specs, check_vma=False)
```

time: 980 us -> 341 us (0.35)
  other arithmetic: 342 us -> 3.8 us
  local copies, waits for them, and re-layouts: 306 us -> 6.92 us
  matrix products: 60.7 us -> 40.8 us
  waiting for transfers between devices: 29.2 us -> 46.7 us
  starting transfers between devices: 153 us -> 165 us
    scatter-add x57 -> x0, other arithmetic: 310 us -> none  [the longest x7 177 us: scatter_local(): jnp.zeros((terms.shape[0], length), jnp.float32).at[:, connect].add(terms)]
    gather x58 -> x0, local copies, waits for them, and re-layouts: 214 us -> none  [the longest x6 68 us: stiff_image(): values = edge_extend(vectors, send_edge)[:, elem_edge]]
    unnamed x119 -> x27, local copies, waits for them, and re-layouts: 34.2 us -> 2.8 us
    transpose x12 -> x0, local copies, waits for them, and re-layouts: 25.9 us -> none  [element_terms(): return jnp.einsum('jke,cke->cje', matrices, values, precision=highest)]
    ppermute x90 -> x84, waiting for transfers between devices: 29.2 us -> 46.7 us  [from_behind(): lax.ppermute(shard, axis, [(i, (i + by) % length) for i in range(length)])]
    dot_general x8 -> x28, matrix products: 55.7 us -> 38.6 us  [the longest x14 25.6 us: gather_cols(): picked = jnp.einsum('rab,nb->ran', split, lo_hot, precision=highest)]
    slice x16, local copies, waits for them, and re-layouts: 18 us -> 1.1 us  [the longest x7 0.52 us: extend(): piece = outgoing[:, direction * ghosts:(direction + 1) * ghosts]]
    unnamed x5 -> x0, other arithmetic: 13.4 us -> none
  transfers between devices with their start and end apart: 90 -> 84, of which waited for: 13 -> 19; matrix products, arithmetic and copies ran while one was open for 35% -> 3% of each run, Pallas kernels for 0% -> 0%
where the time goes in v1:
time: 341 us; the launch traced here: 340 us
  starting transfers between devices  165 us (48%)
  blocking collectives  75.2 us (22%)
  waiting for transfers between devices  46.7 us (14%)
  matrix products  40.8 us (12%)
  local copies, waits for them, and re-layouts  6.92 us (2%)
  other arithmetic  3.8 us (1%)
    ppermute x84, starting transfers between devices, from_behind(): lax.ppermute(shard, axis, [(i, (i + by) % length) for i in range(length)])  165 us
    ppermute x84, waiting for transfers between devices, from_behind(): lax.ppermute(shard, axis, [(i, (i + by) % length) for i in range(length)])  46.7 us
    psum x1, blocking collectives, shards(): lax.psum((jnp.sum(x_block * stiff_x, axis=1), jnp.sum(x_block * mass_x, a...  38.2 us
    psum x1, blocking collectives, shards(): lax.psum(arrange(jnp.stack([stiff_part, mass_part]), w_rows, modes), 'dom')  37 us
    dot_general x14, matrix products, gather_cols(): picked = jnp.einsum('rab,nb->ran', split, lo_hot, precision=highest)  25.6 us
    dot_general x14, matrix products, scatter_cols(): summed = jnp.einsum('ran,nb->rab', spread, lo_hot, precision=highest)  13 us
  transfers between devices with their start and end apart: 84, of which 19 were waited for; matrix products, arithmetic and copies ran while one was open for 3% of the time, Pallas kernels for 0%

profile of v1, /device:TPU:0, one launch (start us, length us, event | category | flops | bytes accessed | tf_op | source)
XLA Modules:
  0.0 340.0 jit_solution(6494226833362064269)
XLA Ops:
  7.7 4.8 %collective-permute-start.3 = (f32[16,64]{1,0:T(8,128)S(1)}, f32[16,64]{1,0:T(8,128)S(1)}, u32[]{:S(2)}, u32[]{:S(2)}) collective-permute-start(f32[16,64]{1,0:T(8,128)S(1)} %get-tuple-element.47), channel_id=1, source_target_pairs={{0,28},{1,29},{2,30},{3,31},{4,0},{5,1},{6,2},{7,3},{8,4},{9,5},{1... | collective-permute-start | bytes 12296 | tf_op jit(solution)/shard_map/ppermute | solution.py:20
  36.0 4.7 %collective-permute-start.8 = (f32[17,64]{1,0:T(8,128)S(1)}, f32[17,64]{1,0:T(8,128)S(1)}, u32[]{:S(2)}, u32[]{:S(2)}) collective-permute-start(f32[17,64]{1,0:T(8,128)S(1)} %get-tuple-element.22), channel_id=1, source_target_pairs={{0,28},{1,29},{2,30},{3,31},{4,0},{5,1},{6,2},{7,3},{8,4},{9,5},{1... | collective-permute-start | bytes 13064 | tf_op jit(solution)/shard_map/ppermute | solution.py:20
  40.8 5.3 %collective-permute-start.6 = (f32[17,64]{1,0:T(8,128)S(1)}, f32[17,64]{1,0:T(8,128)S(1)}, u32[]{:S(2)}, u32[]{:S(2)}) collective-permute-start(f32[17,64]{1,0:T(8,128)S(1)} %get-tuple-element.24), channel_id=1, source_target_pairs={{0,31},{1,0},{2,1},{3,2},{4,3},{5,4},{6,5},{7,6},{8,7},{9,8},{10,9... | collective-permute-start | bytes 13064 | tf_op jit(solution)/shard_map/ppermute | solution.py:20
  49.0 38.2 %all-reduce.2 = (f32[8]{0:T(128)S(1)}, f32[8]{0:T(128)S(1)}) all-reduce(f32[8]{0:T(128)S(1)} %get-tuple-element.6, f32[8]{0:T(128)S(1)} %get-tuple-element.5), channel_id=1, replica_groups=mesh['dom'=32] {'dom'}, use_global_device_ids=true, to_apply=%region_6.7 | all-reduce | flops 16 | bytes 128 | tf_op jit(solution)/shard_map/psum | solution.py:138
  112.2 4.7 %collective-permute-start.20 = (f32[8,64]{1,0:T(8,128)S(1)}, f32[8,64]{1,0:T(8,128)S(1)}, u32[]{:S(2)}, u32[]{:S(2)}) collective-permute-start(f32[8,64]{1,0:T(8,128)S(1)} %get-tuple-element.40), channel_id=1, source_target_pairs={{0,28},{1,29},{2,30},{3,31},{4,0},{5,1},{6,2},{7,3},{8,4},{9,5},{1... | collective-permute-start | bytes 6152 | tf_op jit(solution)/shard_map/ppermute | solution.py:20
  116.9 5.3 %collective-permute-start.18 = (f32[8,64]{1,0:T(8,128)S(1)}, f32[8,64]{1,0:T(8,128)S(1)}, u32[]{:S(2)}, u32[]{:S(2)}) collective-permute-start(f32[8,64]{1,0:T(8,128)S(1)} %get-tuple-element.42), channel_id=1, source_target_pairs={{0,31},{1,0},{2,1},{3,2},{4,3},{5,4},{6,5},{7,6},{8,7},{9,8},{10,9... | collective-permute-start | bytes 6152 | tf_op jit(solution)/shard_map/ppermute | solution.py:20
  129.5 6.9 %collective-permute-start.25 = (f32[8,64]{1,0:T(8,128)S(1)}, f32[8,64]{1,0:T(8,128)S(1)}, u32[]{:S(2)}, u32[]{:S(2)}) collective-permute-start(f32[8,64]{1,0:T(8,128)S(1)} %get-tuple-element.88), channel_id=1, source_target_pairs={{0,31},{1,0},{2,1},{3,2},{4,3},{5,4},{6,5},{7,6},{8,7},{9,8},{10,9... | collective-permute-start | bytes 6152 | tf_op jit(solution)/shard_map/ppermute | solution.py:20
  137.7 5.3 %collective-permute-done.24 = f32[8,64]{1,0:T(8,128)S(1)} collective-permute-done((f32[8,64]{1,0:T(8,128)S(1)}, f32[8,64]{1,0:T(8,128)S(1)}, u32[]{:S(2)}, u32[]{:S(2)}) %collective-permute-start.24) | collective-permute-done | bytes 2080 | tf_op jit(solution)/shard_map/ppermute | solution.py:20
  152.0 4.7 %collective-permute-start.32 = (f32[8,64]{1,0:T(8,128)S(1)}, f32[8,64]{1,0:T(8,128)S(1)}, u32[]{:S(2)}, u32[]{:S(2)}) collective-permute-start(f32[8,64]{1,0:T(8,128)S(1)} %get-tuple-element.34), channel_id=1, source_target_pairs={{0,28},{1,29},{2,30},{3,31},{4,0},{5,1},{6,2},{7,3},{8,4},{9,5},{1... | collective-permute-start | bytes 6152 | tf_op jit(solution)/shard_map/ppermute | solution.py:20
  156.8 5.3 %collective-permute-start.30 = (f32[8,64]{1,0:T(8,128)S(1)}, f32[8,64]{1,0:T(8,128)S(1)}, u32[]{:S(2)}, u32[]{:S(2)}) collective-permute-start(f32[8,64]{1,0:T(8,128)S(1)} %get-tuple-element.36), channel_id=1, source_target_pairs={{0,31},{1,0},{2,1},{3,2},{4,3},{5,4},{6,5},{7,6},{8,7},{9,8},{10,9... | collective-permute-start | bytes 6152 | tf_op jit(solution)/shard_map/ppermute | solution.py:20
  170.1 6.9 %collective-permute-start.37 = (f32[8,64]{1,0:T(8,128)S(1)}, f32[8,64]{1,0:T(8,128)S(1)}, u32[]{:S(2)}, u32[]{:S(2)}) collective-permute-start(f32[8,64]{1,0:T(8,128)S(1)} %get-tuple-element.82), channel_id=1, source_target_pairs={{0,31},{1,0},{2,1},{3,2},{4,3},{5,4},{6,5},{7,6},{8,7},{9,8},{10,9... | collective-permute-start | bytes 6152 | tf_op jit(solution)/shard_map/ppermute | solution.py:20
  180.1 4.7 %collective-permute-start.56 = (f32[1,32]{1,0:T(1,128)S(1)}, f32[1,32]{1,0:T(1,128)S(1)}, u32[]{:S(2)}, u32[]{:S(2)}) collective-permute-start(f32[1,32]{1,0:T(1,128)S(1)} %get-tuple-element.113), channel_id=1, source_target_pairs={{0,28},{1,29},{2,30},{3,31},{4,0},{5,1},{6,2},{7,3},{8,4},{9,5},{1... | collective-permute-start | bytes 392 | tf_op jit(solution)/shard_map/ppermute | solution.py:20
  190.9 5.3 %collective-permute-start.54 = (f32[1,32]{1,0:T(1,128)S(1)}, f32[1,32]{1,0:T(1,128)S(1)}, u32[]{:S(2)}, u32[]{:S(2)}) collective-permute-start(f32[1,32]{1,0:T(1,128)S(1)} %get-tuple-element.115), channel_id=1, source_target_pairs={{0,31},{1,0},{2,1},{3,2},{4,3},{5,4},{6,5},{7,6},{8,7},{9,8},{10,9... | collective-permute-start | bytes 392 | tf_op jit(solution)/shard_map/ppermute | solution.py:20
  197.5 4.6 %collective-permute-start.44 = (f32[8,64]{1,0:T(8,128)S(1)}, f32[8,64]{1,0:T(8,128)S(1)}, u32[]{:S(2)}, u32[]{:S(2)}) collective-permute-start(f32[8,64]{1,0:T(8,128)S(1)} %get-tuple-element.28), channel_id=1, source_target_pairs={{0,28},{1,29},{2,30},{3,31},{4,0},{5,1},{6,2},{7,3},{8,4},{9,5},{1... | collective-permute-start | bytes 6152 | tf_op jit(solution)/shard_map/ppermute | solution.py:20
  202.1 5.3 %collective-permute-start.42 = (f32[8,64]{1,0:T(8,128)S(1)}, f32[8,64]{1,0:T(8,128)S(1)}, u32[]{:S(2)}, u32[]{:S(2)}) collective-permute-start(f32[8,64]{1,0:T(8,128)S(1)} %get-tuple-element.30), channel_id=1, source_target_pairs={{0,31},{1,0},{2,1},{3,2},{4,3},{5,4},{6,5},{7,6},{8,7},{9,8},{10,9... | collective-permute-start | bytes 6152 | tf_op jit(solution)/shard_map/ppermute | solution.py:20
  213.3 4.7 %collective-permute-start.50 = (f32[8,32]{1,0:T(8,128)S(1)}, f32[8,32]{1,0:T(8,128)S(1)}, u32[]{:S(2)}, u32[]{:S(2)}) collective-permute-start(f32[8,32]{1,0:T(8,128)S(1)} %get-tuple-element.60), channel_id=1, source_target_pairs={{0,28},{1,29},{2,30},{3,31},{4,0},{5,1},{6,2},{7,3},{8,4},{9,5},{1... | collective-permute-start | bytes 3080 | tf_op jit(solution)/shard_map/ppermute | solution.py:20
  218.0 5.3 %collective-permute-start.48 = (f32[8,32]{1,0:T(8,128)S(1)}, f32[8,32]{1,0:T(8,128)S(1)}, u32[]{:S(2)}, u32[]{:S(2)}) collective-permute-start(f32[8,32]{1,0:T(8,128)S(1)} %get-tuple-element.62), channel_id=1, source_target_pairs={{0,31},{1,0},{2,1},{3,2},{4,3},{5,4},{6,5},{7,6},{8,7},{9,8},{10,9... | collective-permute-start | bytes 3080 | tf_op jit(solution)/shard_map/ppermute | solution.py:20
  230.4 6.9 %collective-permute-start.61 = (f32[8,32]{1,0:T(8,128)S(1)}, f32[8,32]{1,0:T(8,128)S(1)}, u32[]{:S(2)}, u32[]{:S(2)}) collective-permute-start(f32[8,32]{1,0:T(8,128)S(1)} %get-tuple-element.108), channel_id=1, source_target_pairs={{0,31},{1,0},{2,1},{3,2},{4,3},{5,4},{6,5},{7,6},{8,7},{9,8},{10,9... | collective-permute-start | bytes 3080 | tf_op jit(solution)/shard_map/ppermute | solution.py:20
  238.6 5.3 %collective-permute-done.60 = f32[8,32]{1,0:T(8,128)S(1)} collective-permute-done((f32[8,32]{1,0:T(8,128)S(1)}, f32[8,32]{1,0:T(8,128)S(1)}, u32[]{:S(2)}, u32[]{:S(2)}) %collective-permute-start.60) | collective-permute-done | bytes 1056 | tf_op jit(solution)/shard_map/ppermute | solution.py:20
  249.6 4.7 %collective-permute-start.68 = (f32[8,32]{1,0:T(8,128)S(1)}, f32[8,32]{1,0:T(8,128)S(1)}, u32[]{:S(2)}, u32[]{:S(2)}) collective-permute-start(f32[8,32]{1,0:T(8,128)S(1)} %get-tuple-element.54), channel_id=1, source_target_pairs={{0,28},{1,29},{2,30},{3,31},{4,0},{5,1},{6,2},{7,3},{8,4},{9,5},{1... | collective-permute-start | bytes 3080 | tf_op jit(solution)/shard_map/ppermute | solution.py:20
  254.3 5.3 %collective-permute-start.66 = (f32[8,32]{1,0:T(8,128)S(1)}, f32[8,32]{1,0:T(8,128)S(1)}, u32[]{:S(2)}, u32[]{:S(2)}) collective-permute-start(f32[8,32]{1,0:T(8,128)S(1)} %get-tuple-element.56), channel_id=1, source_target_pairs={{0,31},{1,0},{2,1},{3,2},{4,3},{5,4},{6,5},{7,6},{8,7},{9,8},{10,9... | collective-permute-start | bytes 3080 | tf_op jit(solution)/shard_map/ppermute | solution.py:20
  266.7 6.9 %collective-permute-start.73 = (f32[8,32]{1,0:T(8,128)S(1)}, f32[8,32]{1,0:T(8,128)S(1)}, u32[]{:S(2)}, u32[]{:S(2)}) collective-permute-start(f32[8,32]{1,0:T(8,128)S(1)} %get-tuple-element.102), channel_id=1, source_target_pairs={{0,31},{1,0},{2,1},{3,2},{4,3},{5,4},{6,5},{7,6},{8,7},{9,8},{10,9... | collective-permute-start | bytes 3080 | tf_op jit(solution)/shard_map/ppermute | solution.py:20
  274.9 5.3 %collective-permute-done.72 = f32[8,32]{1,0:T(8,128)S(1)} collective-permute-done((f32[8,32]{1,0:T(8,128)S(1)}, f32[8,32]{1,0:T(8,128)S(1)}, u32[]{:S(2)}, u32[]{:S(2)}) %collective-permute-start.72) | collective-permute-done | bytes 1056 | tf_op jit(solution)/shard_map/ppermute | solution.py:20
  302.3 37.0 %psum.23 = f32[2,24,24]{2,1,0:T(8,128)S(1)} all-reduce(f32[2,24,24]{2,1,0:T(8,128)S(1)} %fusion.183), channel_id=1, replica_groups=mesh['dom'=32] {'dom'}, use_global_device_ids=true, to_apply=%region_28.29 | all-reduce | flops 1152 | bytes 9216 | tf_op jit(solution)/shard_map/psum | solution.py:181
  (284 shorter events, 144.6 us)
Async XLA Ops:
  3.6 13.0 %collective-permute-start.5 = (f32[16,64]{1,0:T(8,128)S(1)}, f32[16,64]{1,0:T(8,128)S(1)}, u32[]{:S(2)}, u32[]{:S(2)}) collective-permute-start(f32[16,64]{1,0:T(8,128)S(1)} %get-tuple-element.45), channel_id=1, source_target_pairs={{0,16},{1,17},{2,18},{3,19},{4,20},{5,21},{6,22},{7,23},{8,24},{9,... | collective-permute-start | bytes 12296 | tf_op jit(solution)/shard_map/ppermute | solution.py:20
  33.1 13.0 %collective-permute-start.10 = (f32[17,64]{1,0:T(8,128)S(1)}, f32[17,64]{1,0:T(8,128)S(1)}, u32[]{:S(2)}, u32[]{:S(2)}) collective-permute-start(f32[17,64]{1,0:T(8,128)S(1)} %get-tuple-element.20), channel_id=1, source_target_pairs={{0,16},{1,17},{2,18},{3,19},{4,20},{5,21},{6,22},{7,23},{8,24},{9,... | collective-permute-start | bytes 13064 | tf_op jit(solution)/shard_map/ppermute | solution.py:20
  109.2 13.1 %collective-permute-start.22 = (f32[8,64]{1,0:T(8,128)S(1)}, f32[8,64]{1,0:T(8,128)S(1)}, u32[]{:S(2)}, u32[]{:S(2)}) collective-permute-start(f32[8,64]{1,0:T(8,128)S(1)} %get-tuple-element.38), channel_id=1, source_target_pairs={{0,16},{1,17},{2,18},{3,19},{4,20},{5,21},{6,22},{7,23},{8,24},{9,... | collective-permute-start | bytes 6152 | tf_op jit(solution)/shard_map/ppermute | solution.py:20
  124.5 11.9 %collective-permute-start.29 = (f32[8,64]{1,0:T(8,128)S(1)}, f32[8,64]{1,0:T(8,128)S(1)}, u32[]{:S(2)}, u32[]{:S(2)}) collective-permute-start(f32[8,64]{1,0:T(8,128)S(1)} %get-tuple-element.84), channel_id=1, source_target_pairs={{0,16},{1,17},{2,18},{3,19},{4,20},{5,21},{6,22},{7,23},{8,24},{9,... | collective-permute-start | bytes 6152 | tf_op jit(solution)/shard_map/ppermute | solution.py:20
  124.5 11.9 %collective-permute-start.28 = (f32[8,64]{1,0:T(8,128)S(1)}, f32[8,64]{1,0:T(8,128)S(1)}, u32[]{:S(2)}, u32[]{:S(2)}) collective-permute-start(f32[8,64]{1,0:T(8,128)S(1)} %get-tuple-element.85), channel_id=1, source_target_pairs={{0,16},{1,17},{2,18},{3,19},{4,20},{5,21},{6,22},{7,23},{8,24},{9,... | collective-permute-start | bytes 6152 | tf_op jit(solution)/shard_map/ppermute | solution.py:20
  149.1 13.1 %collective-permute-start.34 = (f32[8,64]{1,0:T(8,128)S(1)}, f32[8,64]{1,0:T(8,128)S(1)}, u32[]{:S(2)}, u32[]{:S(2)}) collective-permute-start(f32[8,64]{1,0:T(8,128)S(1)} %get-tuple-element.32), channel_id=1, source_target_pairs={{0,16},{1,17},{2,18},{3,19},{4,20},{5,21},{6,22},{7,23},{8,24},{9,... | collective-permute-start | bytes 6152 | tf_op jit(solution)/shard_map/ppermute | solution.py:20
  152.0 10.2 %collective-permute-start.33 = (f32[8,64]{1,0:T(8,128)S(1)}, f32[8,64]{1,0:T(8,128)S(1)}, u32[]{:S(2)}, u32[]{:S(2)}) collective-permute-start(f32[8,64]{1,0:T(8,128)S(1)} %get-tuple-element.33), channel_id=1, source_target_pairs={{0,4},{1,5},{2,6},{3,7},{4,8},{5,9},{6,10},{7,11},{8,12},{9,13},{1... | collective-permute-start | bytes 6152 | tf_op jit(solution)/shard_map/ppermute | solution.py:20
  152.0 10.2 %collective-permute-start.32 = (f32[8,64]{1,0:T(8,128)S(1)}, f32[8,64]{1,0:T(8,128)S(1)}, u32[]{:S(2)}, u32[]{:S(2)}) collective-permute-start(f32[8,64]{1,0:T(8,128)S(1)} %get-tuple-element.34), channel_id=1, source_target_pairs={{0,28},{1,29},{2,30},{3,31},{4,0},{5,1},{6,2},{7,3},{8,4},{9,5},{1... | collective-permute-start | bytes 6152 | tf_op jit(solution)/shard_map/ppermute | solution.py:20
  164.3 12.6 %collective-permute-start.41 = (f32[8,64]{1,0:T(8,128)S(1)}, f32[8,64]{1,0:T(8,128)S(1)}, u32[]{:S(2)}, u32[]{:S(2)}) collective-permute-start(f32[8,64]{1,0:T(8,128)S(1)} %get-tuple-element.78), channel_id=1, source_target_pairs={{0,16},{1,17},{2,18},{3,19},{4,20},{5,21},{6,22},{7,23},{8,24},{9,... | collective-permute-start | bytes 6152 | tf_op jit(solution)/shard_map/ppermute | solution.py:20
  165.1 12.0 %collective-permute-start.40 = (f32[8,64]{1,0:T(8,128)S(1)}, f32[8,64]{1,0:T(8,128)S(1)}, u32[]{:S(2)}, u32[]{:S(2)}) collective-permute-start(f32[8,64]{1,0:T(8,128)S(1)} %get-tuple-element.79), channel_id=1, source_target_pairs={{0,16},{1,17},{2,18},{3,19},{4,20},{5,21},{6,22},{7,23},{8,24},{9,... | collective-permute-start | bytes 6152 | tf_op jit(solution)/shard_map/ppermute | solution.py:20
  168.0 12.0 %collective-permute-start.38 = (f32[8,64]{1,0:T(8,128)S(1)}, f32[8,64]{1,0:T(8,128)S(1)}, u32[]{:S(2)}, u32[]{:S(2)}) collective-permute-start(f32[8,64]{1,0:T(8,128)S(1)} %get-tuple-element.81), channel_id=1, source_target_pairs={{0,4},{1,5},{2,6},{3,7},{4,8},{5,9},{6,10},{7,11},{8,12},{9,13},{1... | collective-permute-start | bytes 6152 | tf_op jit(solution)/shard_map/ppermute | solution.py:20
  177.1 13.8 %collective-permute-start.59 = (f32[1,32]{1,0:T(1,128)S(1)}, f32[1,32]{1,0:T(1,128)S(1)}, u32[]{:S(2)}, u32[]{:S(2)}) collective-permute-start(f32[1,32]{1,0:T(1,128)S(1)} %get-tuple-element.110), channel_id=1, source_target_pairs={{0,16},{1,17},{2,18},{3,19},{4,20},{5,21},{6,22},{7,23},{8,24},{9,... | collective-permute-start | bytes 392 | tf_op jit(solution)/shard_map/ppermute | solution.py:20
  177.1 13.8 %collective-permute-start.58 = (f32[1,32]{1,0:T(1,128)S(1)}, f32[1,32]{1,0:T(1,128)S(1)}, u32[]{:S(2)}, u32[]{:S(2)}) collective-permute-start(f32[1,32]{1,0:T(1,128)S(1)} %get-tuple-element.111), channel_id=1, source_target_pairs={{0,16},{1,17},{2,18},{3,19},{4,20},{5,21},{6,22},{7,23},{8,24},{9,... | collective-permute-start | bytes 392 | tf_op jit(solution)/shard_map/ppermute | solution.py:20
  180.0 16.2 %collective-permute-start.57 = (f32[1,32]{1,0:T(1,128)S(1)}, f32[1,32]{1,0:T(1,128)S(1)}, u32[]{:S(2)}, u32[]{:S(2)}) collective-permute-start(f32[1,32]{1,0:T(1,128)S(1)} %get-tuple-element.112), channel_id=1, source_target_pairs={{0,4},{1,5},{2,6},{3,7},{4,8},{5,9},{6,10},{7,11},{8,12},{9,13},{1... | collective-permute-start | bytes 392 | tf_op jit(solution)/shard_map/ppermute | solution.py:20
  180.1 17.3 %collective-permute-start.56 = (f32[1,32]{1,0:T(1,128)S(1)}, f32[1,32]{1,0:T(1,128)S(1)}, u32[]{:S(2)}, u32[]{:S(2)}) collective-permute-start(f32[1,32]{1,0:T(1,128)S(1)} %get-tuple-element.113), channel_id=1, source_target_pairs={{0,28},{1,29},{2,30},{3,31},{4,0},{5,1},{6,2},{7,3},{8,4},{9,5},{1... | collective-permute-start | bytes 392 | tf_op jit(solution)/shard_map/ppermute | solution.py:20
  190.8 11.3 %collective-permute-start.47 = (f32[8,64]{1,0:T(8,128)S(1)}, f32[8,64]{1,0:T(8,128)S(1)}, u32[]{:S(2)}, u32[]{:S(2)}) collective-permute-start(f32[8,64]{1,0:T(8,128)S(1)} %get-tuple-element.25), channel_id=1, source_target_pairs={{0,16},{1,17},{2,18},{3,19},{4,20},{5,21},{6,22},{7,23},{8,24},{9,... | collective-permute-start | bytes 6152 | tf_op jit(solution)/shard_map/ppermute | solution.py:20
  190.9 11.2 %collective-permute-start.54 = (f32[1,32]{1,0:T(1,128)S(1)}, f32[1,32]{1,0:T(1,128)S(1)}, u32[]{:S(2)}, u32[]{:S(2)}) collective-permute-start(f32[1,32]{1,0:T(1,128)S(1)} %get-tuple-element.115), channel_id=1, source_target_pairs={{0,31},{1,0},{2,1},{3,2},{4,3},{5,4},{6,5},{7,6},{8,7},{9,8},{10,9... | collective-permute-start | bytes 392 | tf_op jit(solution)/shard_map/ppermute | solution.py:20
  196.3 11.3 %collective-permute-start.46 = (f32[8,64]{1,0:T(8,128)S(1)}, f32[8,64]{1,0:T(8,128)S(1)}, u32[]{:S(2)}, u32[]{:S(2)}) collective-permute-start(f32[8,64]{1,0:T(8,128)S(1)} %get-tuple-element.26), channel_id=1, source_target_pairs={{0,16},{1,17},{2,18},{3,19},{4,20},{5,21},{6,22},{7,23},{8,24},{9,... | collective-permute-start | bytes 6152 | tf_op jit(solution)/shard_map/ppermute | solution.py:20
  210.4 13.0 %collective-permute-start.52 = (f32[8,32]{1,0:T(8,128)S(1)}, f32[8,32]{1,0:T(8,128)S(1)}, u32[]{:S(2)}, u32[]{:S(2)}) collective-permute-start(f32[8,32]{1,0:T(8,128)S(1)} %get-tuple-element.58), channel_id=1, source_target_pairs={{0,16},{1,17},{2,18},{3,19},{4,20},{5,21},{6,22},{7,23},{8,24},{9,... | collective-permute-start | bytes 3080 | tf_op jit(solution)/shard_map/ppermute | solution.py:20
  225.4 11.8 %collective-permute-start.65 = (f32[8,32]{1,0:T(8,128)S(1)}, f32[8,32]{1,0:T(8,128)S(1)}, u32[]{:S(2)}, u32[]{:S(2)}) collective-permute-start(f32[8,32]{1,0:T(8,128)S(1)} %get-tuple-element.104), channel_id=1, source_target_pairs={{0,16},{1,17},{2,18},{3,19},{4,20},{5,21},{6,22},{7,23},{8,24},{9,... | collective-permute-start | bytes 3080 | tf_op jit(solution)/shard_map/ppermute | solution.py:20
  225.4 11.8 %collective-permute-start.64 = (f32[8,32]{1,0:T(8,128)S(1)}, f32[8,32]{1,0:T(8,128)S(1)}, u32[]{:S(2)}, u32[]{:S(2)}) collective-permute-start(f32[8,32]{1,0:T(8,128)S(1)} %get-tuple-element.105), channel_id=1, source_target_pairs={{0,16},{1,17},{2,18},{3,19},{4,20},{5,21},{6,22},{7,23},{8,24},{9,... | collective-permute-start | bytes 3080 | tf_op jit(solution)/shard_map/ppermute | solution.py:20
  246.7 13.0 %collective-permute-start.70 = (f32[8,32]{1,0:T(8,128)S(1)}, f32[8,32]{1,0:T(8,128)S(1)}, u32[]{:S(2)}, u32[]{:S(2)}) collective-permute-start(f32[8,32]{1,0:T(8,128)S(1)} %get-tuple-element.52), channel_id=1, source_target_pairs={{0,16},{1,17},{2,18},{3,19},{4,20},{5,21},{6,22},{7,23},{8,24},{9,... | collective-permute-start | bytes 3080 | tf_op jit(solution)/shard_map/ppermute | solution.py:20
  261.7 11.9 %collective-permute-start.77 = (f32[8,32]{1,0:T(8,128)S(1)}, f32[8,32]{1,0:T(8,128)S(1)}, u32[]{:S(2)}, u32[]{:S(2)}) collective-permute-start(f32[8,32]{1,0:T(8,128)S(1)} %get-tuple-element.98), channel_id=1, source_target_pairs={{0,16},{1,17},{2,18},{3,19},{4,20},{5,21},{6,22},{7,23},{8,24},{9,... | collective-permute-start | bytes 3080 | tf_op jit(solution)/shard_map/ppermute | solution.py:20
  261.7 12.4 %collective-permute-start.76 = (f32[8,32]{1,0:T(8,128)S(1)}, f32[8,32]{1,0:T(8,128)S(1)}, u32[]{:S(2)}, u32[]{:S(2)}) collective-permute-start(f32[8,32]{1,0:T(8,128)S(1)} %get-tuple-element.99), channel_id=1, source_target_pairs={{0,16},{1,17},{2,18},{3,19},{4,20},{5,21},{6,22},{7,23},{8,24},{9,... | collective-permute-start | bytes 3080 | tf_op jit(solution)/shard_map/ppermute | solution.py:20
  (69 other events, 557.3 us)

commit v2 on v1

--- a/solution.py
+++ b/solution.py
@@ -18,6 +18,33 @@
 def from_behind(shard, axis, by):
     length = lax.axis_size(axis)
     return lax.ppermute(shard, axis, [(i, (i + by) % length) for i in range(length)])
+
+
+def shift_pieces(pieces, offsets):
+    length = lax.axis_size("dom")
+    out = [None] * len(pieces)
+    targets = {}
+    for number, offset in enumerate(offsets):
+        targets.setdefault(offset % length, []).append(number)
+    for offset, numbers in targets.items():
+        sizes = [pieces[number].shape[1] for number in numbers]
+        moved = from_behind(jnp.concatenate([pieces[number] for number in numbers], axis=1), "dom", offset)
+        start = 0
+        for number, size in zip(numbers, sizes):
+            out[number] = moved[:, start : start + size]
+            start += size
+    return out
+
+
+def all_sum(value):
+    length = lax.axis_size("dom")
+    if length & (length - 1):
+        return lax.psum(value, "dom")
+    stride = 1
+    while stride < length:
+        value = value + lax.ppermute(value, "dom", [(i, i ^ stride) for i in range(length)])
+        stride *= 2
+    return value
 
 
 def index_table(index, length):
@@ -51,20 +78,15 @@
 def extend(values, send_table):
     outgoing = gather_cols(values, send_table)
     ghosts = outgoing.shape[1] // 6
-    pieces = [values]
-    for direction in range(6):
-        piece = outgoing[:, direction * ghosts : (direction + 1) * ghosts]
-        pieces.append(from_behind(piece, "dom", OFFSETS[direction]))
-    return jnp.concatenate(pieces, axis=1)
+    pieces = [outgoing[:, direction * ghosts : (direction + 1) * ghosts] for direction in range(6)]
+    return jnp.concatenate([values] + shift_pieces(pieces, OFFSETS), axis=1)
 
 
 def give_back(extended, send_table):
     owned = send_table[2]
     ghosts = (extended.shape[1] - owned) // 6
-    backs = []
-    for direction in range(6):
-        start = owned + direction * ghosts
-        backs.append(from_behind(extended[:, start : start + ghosts], "dom", -OFFSETS[direction]))
+    pieces = [extended[:, owned + d * ghosts : owned + (d + 1) * ghosts] for d in range(6)]
+    backs = shift_pieces(pieces, [-offset for offset in OFFSETS])
     return extended[:, :owned] + scatter_cols(jnp.concatenate(backs, axis=1), send_table)
 
 
@@ -135,8 +157,8 @@
     edge_diag = images[2 * modes]
     node_diag_terms = jnp.einsum("jje->je", node_elem).reshape(1, -1)
     node_diag = give_back(scatter_cols(node_diag_terms, node_table), send_node_table)[0]
-    numerator, denominator = lax.psum(
-        (jnp.sum(x_block * stiff_x, axis=1), jnp.sum(x_block * mass_x, axis=1)), "dom"
+    numerator, denominator = all_sum(
+        jnp.stack([jnp.sum(x_block * stiff_x, axis=1), jnp.sum(x_block * mass_x, axis=1)])
     )
     quotient = numerator / denominator
     residual = stiff_x - quotient[:, None] * mass_x
@@ -178,7 +200,7 @@
     )
     stiff_part = inner_elements(pair_values, stiff_pair)
     mass_part = inner_elements(pair_values, mass_pair)
-    full_gram = lax.psum(arrange(jnp.stack([stiff_part, mass_part]), w_rows, modes), "dom")
+    full_gram = all_sum(arrange(jnp.stack([stiff_part, mass_part]), w_rows, modes))
     total_edges = owned_edges * lax.axis_size("dom")
     return (w_block, full_gram[0] / total_edges, full_gram[1] / total_edges)
 

time: 341 us -> 263 us (0.77)
  blocking collectives: 75.2 us -> 0 us
  starting transfers between devices: 165 us -> 128 us
  waiting for transfers between devices: 46.7 us -> 81.1 us
    psum x2 -> x0, blocking collectives: 75.2 us -> none  [the longest x1 38.2 us: shards(): lax.psum((jnp.sum(x_block * stiff_x, axis=1), jnp.sum(x_block * mass_x, a...]
    ppermute x84 -> x70, starting transfers between devices: 165 us -> 126 us  [from_behind(): lax.ppermute(shard, axis, [(i, (i + by) % length) for i in range(length)])]
    ppermute x0 -> x10, waiting for transfers between devices: none -> 32.5 us  [all_sum(): lax.ppermute(value, 'dom', [(i, i ^ stride) for i in range(length)])]
    ppermute x84 -> x70, waiting for transfers between devices: 46.7 us -> 48.7 us  [from_behind(): lax.ppermute(shard, axis, [(i, (i + by) % length) for i in range(length)])]
  transfers between devices with their start and end apart: 84 -> 80, of which waited for: 19 -> 30; matrix products, arithmetic and copies ran while one was open for 3% -> 1% of each run, Pallas kernels for 0% -> 0%
where the time goes in v2:
time: 263 us; the launch traced here: 262 us
  starting transfers between devices  128 us (49%)
  waiting for transfers between devices  81.1 us (31%)
  matrix products  40.8 us (16%)
  local copies, waits for them, and re-layouts  7.36 us (3%)
  other arithmetic  3.87 us (1%)
    ppermute x70, starting transfers between devices, from_behind(): lax.ppermute(shard, axis, [(i, (i + by) % length) for i in range(length)])  126 us
    ppermute x70, waiting for transfers between devices, from_behind(): lax.ppermute(shard, axis, [(i, (i + by) % length) for i in range(length)])  48.7 us
    ppermute x10, waiting for transfers between devices, all_sum(): lax.ppermute(value, 'dom', [(i, i ^ stride) for i in range(length)])  32.5 us
    dot_general x14, matrix products, gather_cols(): picked = jnp.einsum('rab,nb->ran', split, lo_hot, precision=highest)  25.6 us
    dot_general x14, matrix products, scatter_cols(): summed = jnp.einsum('ran,nb->rab', spread, lo_hot, precision=highest)  13 us
  transfers between devices with their start and end apart: 80, of which 30 were waited for; matrix products, arithmetic and copies ran while one was open for 1% of the time, Pallas kernels for 0%

profile of v2, /device:TPU:0, one launch (start us, length us, event | category | flops | bytes accessed | tf_op | source)
XLA Modules:
  0.0 262.4 jit_solution(11764989776770234756)
XLA Ops:
  3.5 6.0 %collective-permute-start.3 = (f32[16,64]{1,0:T(8,128)S(1)}, f32[16,64]{1,0:T(8,128)S(1)}, u32[]{:S(2)}, u32[]{:S(2)}) collective-permute-start(f32[16,64]{1,0:T(8,128)S(1)} %get-tuple-element.35), channel_id=1, source_target_pairs={{0,28},{1,29},{2,30},{3,31},{4,0},{5,1},{6,2},{7,3},{8,4},{9,5},{1... | collective-permute-start | bytes 12296 | tf_op jit(solution)/shard_map/ppermute | solution.py:20
  15.9 4.9 %collective-permute-done = f32[16,64]{1,0:T(8,128)S(1)} collective-permute-done((f32[16,64]{1,0:T(8,128)S(1)}, f32[16,64]{1,0:T(8,128)S(1)}, u32[]{:S(2)}, u32[]{:S(2)}) %collective-permute-start) | collective-permute-done | bytes 4128 | tf_op jit(solution)/shard_map/ppermute | solution.py:20
  30.6 4.7 %collective-permute-start.7 = (f32[17,64]{1,0:T(8,128)S(1)}, f32[17,64]{1,0:T(8,128)S(1)}, u32[]{:S(2)}, u32[]{:S(2)}) collective-permute-start(f32[17,64]{1,0:T(8,128)S(1)} %get-tuple-element.18), channel_id=1, source_target_pairs={{0,28},{1,29},{2,30},{3,31},{4,0},{5,1},{6,2},{7,3},{8,4},{9,5},{1... | collective-permute-start | bytes 13064 | tf_op jit(solution)/shard_map/ppermute | solution.py:20
  35.3 5.3 %collective-permute-start.5 = (f32[17,64]{1,0:T(8,128)S(1)}, f32[17,64]{1,0:T(8,128)S(1)}, u32[]{:S(2)}, u32[]{:S(2)}) collective-permute-start(f32[17,64]{1,0:T(8,128)S(1)} %get-tuple-element.20), channel_id=1, source_target_pairs={{0,31},{1,0},{2,1},{3,2},{4,3},{5,4},{6,5},{7,6},{8,7},{9,8},{10,9... | collective-permute-start | bytes 13064 | tf_op jit(solution)/shard_map/ppermute | solution.py:20
  65.9 5.0 %collective-permute-done.17 = f32[8,64]{1,0:T(8,128)S(1)} collective-permute-done((f32[8,64]{1,0:T(8,128)S(1)}, f32[8,64]{1,0:T(8,128)S(1)}, u32[]{:S(2)}, u32[]{:S(2)}) %collective-permute-start.17) | collective-permute-done | bytes 2080 | tf_op jit(solution)/shard_map/ppermute | solution.py:20
  78.3 4.7 %collective-permute-start.22 = (f32[8,64]{1,0:T(8,128)S(1)}, f32[8,64]{1,0:T(8,128)S(1)}, u32[]{:S(2)}, u32[]{:S(2)}) collective-permute-start(f32[8,64]{1,0:T(8,128)S(1)} %get-tuple-element.30), channel_id=1, source_target_pairs={{0,28},{1,29},{2,30},{3,31},{4,0},{5,1},{6,2},{7,3},{8,4},{9,5},{1... | collective-permute-start | bytes 6152 | tf_op jit(solution)/shard_map/ppermute | solution.py:20
  83.0 5.3 %collective-permute-start.20 = (f32[8,64]{1,0:T(8,128)S(1)}, f32[8,64]{1,0:T(8,128)S(1)}, u32[]{:S(2)}, u32[]{:S(2)}) collective-permute-start(f32[8,64]{1,0:T(8,128)S(1)} %get-tuple-element.32), channel_id=1, source_target_pairs={{0,31},{1,0},{2,1},{3,2},{4,3},{5,4},{6,5},{7,6},{8,7},{9,8},{10,9... | collective-permute-start | bytes 6152 | tf_op jit(solution)/shard_map/ppermute | solution.py:20
  92.6 7.4 %collective-permute-start.26 = (f32[8,64]{1,0:T(8,128)S(1)}, f32[8,64]{1,0:T(8,128)S(1)}, u32[]{:S(2)}, u32[]{:S(2)}) collective-permute-start(f32[8,64]{1,0:T(8,128)S(1)} %get-tuple-element.66), channel_id=1, source_target_pairs={{0,31},{1,0},{2,1},{3,2},{4,3},{5,4},{6,5},{7,6},{8,7},{9,8},{10,9... | collective-permute-start | bytes 6152 | tf_op jit(solution)/shard_map/ppermute | solution.py:20
  101.4 5.3 %collective-permute-done.25 = f32[8,64]{1,0:T(8,128)S(1)} collective-permute-done((f32[8,64]{1,0:T(8,128)S(1)}, f32[8,64]{1,0:T(8,128)S(1)}, u32[]{:S(2)}, u32[]{:S(2)}) %collective-permute-start.25) | collective-permute-done | bytes 2080 | tf_op jit(solution)/shard_map/ppermute | solution.py:20
  112.8 4.7 %collective-permute-start.32 = (f32[8,64]{1,0:T(8,128)S(1)}, f32[8,64]{1,0:T(8,128)S(1)}, u32[]{:S(2)}, u32[]{:S(2)}) collective-permute-start(f32[8,64]{1,0:T(8,128)S(1)} %get-tuple-element.26), channel_id=1, source_target_pairs={{0,28},{1,29},{2,30},{3,31},{4,0},{5,1},{6,2},{7,3},{8,4},{9,5},{1... | collective-permute-start | bytes 6152 | tf_op jit(solution)/shard_map/ppermute | solution.py:20
  117.5 5.3 %collective-permute-start.30 = (f32[8,64]{1,0:T(8,128)S(1)}, f32[8,64]{1,0:T(8,128)S(1)}, u32[]{:S(2)}, u32[]{:S(2)}) collective-permute-start(f32[8,64]{1,0:T(8,128)S(1)} %get-tuple-element.28), channel_id=1, source_target_pairs={{0,31},{1,0},{2,1},{3,2},{4,3},{5,4},{6,5},{7,6},{8,7},{9,8},{10,9... | collective-permute-start | bytes 6152 | tf_op jit(solution)/shard_map/ppermute | solution.py:20
  127.7 5.3 %collective-permute-start.50 = (f32[1,32]{1,0:T(1,128)S(1)}, f32[1,32]{1,0:T(1,128)S(1)}, u32[]{:S(2)}, u32[]{:S(2)}) collective-permute-start(f32[1,32]{1,0:T(1,128)S(1)} %get-tuple-element.85), channel_id=1, source_target_pairs={{0,31},{1,0},{2,1},{3,2},{4,3},{5,4},{6,5},{7,6},{8,7},{9,8},{10,9... | collective-permute-start | bytes 392 | tf_op jit(solution)/shard_map/ppermute | solution.py:20
  151.0 4.7 %collective-permute-start.42 = (f32[8,64]{1,0:T(8,128)S(1)}, f32[8,64]{1,0:T(8,128)S(1)}, u32[]{:S(2)}, u32[]{:S(2)}) collective-permute-start(f32[8,64]{1,0:T(8,128)S(1)} %get-tuple-element.22), channel_id=1, source_target_pairs={{0,28},{1,29},{2,30},{3,31},{4,0},{5,1},{6,2},{7,3},{8,4},{9,5},{1... | collective-permute-start | bytes 6152 | tf_op jit(solution)/shard_map/ppermute | solution.py:20
  155.7 5.3 %collective-permute-start.40 = (f32[8,64]{1,0:T(8,128)S(1)}, f32[8,64]{1,0:T(8,128)S(1)}, u32[]{:S(2)}, u32[]{:S(2)}) collective-permute-start(f32[8,64]{1,0:T(8,128)S(1)} %get-tuple-element.24), channel_id=1, source_target_pairs={{0,31},{1,0},{2,1},{3,2},{4,3},{5,4},{6,5},{7,6},{8,7},{9,8},{10,9... | collective-permute-start | bytes 6152 | tf_op jit(solution)/shard_map/ppermute | solution.py:20
  163.8 4.7 %collective-permute-start.47 = (f32[8,32]{1,0:T(8,128)S(1)}, f32[8,32]{1,0:T(8,128)S(1)}, u32[]{:S(2)}, u32[]{:S(2)}) collective-permute-start(f32[8,32]{1,0:T(8,128)S(1)} %get-tuple-element.44), channel_id=1, source_target_pairs={{0,28},{1,29},{2,30},{3,31},{4,0},{5,1},{6,2},{7,3},{8,4},{9,5},{1... | collective-permute-start | bytes 3080 | tf_op jit(solution)/shard_map/ppermute | solution.py:20
  168.5 5.3 %collective-permute-start.45 = (f32[8,32]{1,0:T(8,128)S(1)}, f32[8,32]{1,0:T(8,128)S(1)}, u32[]{:S(2)}, u32[]{:S(2)}) collective-permute-start(f32[8,32]{1,0:T(8,128)S(1)} %get-tuple-element.46), channel_id=1, source_target_pairs={{0,31},{1,0},{2,1},{3,2},{4,3},{5,4},{6,5},{7,6},{8,7},{9,8},{10,9... | collective-permute-start | bytes 3080 | tf_op jit(solution)/shard_map/ppermute | solution.py:20
  177.9 7.4 %collective-permute-start.56 = (f32[8,32]{1,0:T(8,128)S(1)}, f32[8,32]{1,0:T(8,128)S(1)}, u32[]{:S(2)}, u32[]{:S(2)}) collective-permute-start(f32[8,32]{1,0:T(8,128)S(1)} %get-tuple-element.80), channel_id=1, source_target_pairs={{0,31},{1,0},{2,1},{3,2},{4,3},{5,4},{6,5},{7,6},{8,7},{9,8},{10,9... | collective-permute-start | bytes 3080 | tf_op jit(solution)/shard_map/ppermute | solution.py:20
  186.7 5.3 %collective-permute-done.55 = f32[8,32]{1,0:T(8,128)S(1)} collective-permute-done((f32[8,32]{1,0:T(8,128)S(1)}, f32[8,32]{1,0:T(8,128)S(1)}, u32[]{:S(2)}, u32[]{:S(2)}) %collective-permute-start.55) | collective-permute-done | bytes 1056 | tf_op jit(solution)/shard_map/ppermute | solution.py:20
  194.9 4.7 %collective-permute-start.62 = (f32[8,32]{1,0:T(8,128)S(1)}, f32[8,32]{1,0:T(8,128)S(1)}, u32[]{:S(2)}, u32[]{:S(2)}) collective-permute-start(f32[8,32]{1,0:T(8,128)S(1)} %get-tuple-element.40), channel_id=1, source_target_pairs={{0,28},{1,29},{2,30},{3,31},{4,0},{5,1},{6,2},{7,3},{8,4},{9,5},{1... | collective-permute-start | bytes 3080 | tf_op jit(solution)/shard_map/ppermute | solution.py:20
  199.6 5.3 %collective-permute-start.60 = (f32[8,32]{1,0:T(8,128)S(1)}, f32[8,32]{1,0:T(8,128)S(1)}, u32[]{:S(2)}, u32[]{:S(2)}) collective-permute-start(f32[8,32]{1,0:T(8,128)S(1)} %get-tuple-element.42), channel_id=1, source_target_pairs={{0,31},{1,0},{2,1},{3,2},{4,3},{5,4},{6,5},{7,6},{8,7},{9,8},{10,9... | collective-permute-start | bytes 3080 | tf_op jit(solution)/shard_map/ppermute | solution.py:20
  209.0 7.4 %collective-permute-start.66 = (f32[8,32]{1,0:T(8,128)S(1)}, f32[8,32]{1,0:T(8,128)S(1)}, u32[]{:S(2)}, u32[]{:S(2)}) collective-permute-start(f32[8,32]{1,0:T(8,128)S(1)} %get-tuple-element.76), channel_id=1, source_target_pairs={{0,31},{1,0},{2,1},{3,2},{4,3},{5,4},{6,5},{7,6},{8,7},{9,8},{10,9... | collective-permute-start | bytes 3080 | tf_op jit(solution)/shard_map/ppermute | solution.py:20
  217.8 5.3 %collective-permute-done.65 = f32[8,32]{1,0:T(8,128)S(1)} collective-permute-done((f32[8,32]{1,0:T(8,128)S(1)}, f32[8,32]{1,0:T(8,128)S(1)}, u32[]{:S(2)}, u32[]{:S(2)}) %collective-permute-start.65) | collective-permute-done | bytes 1056 | tf_op jit(solution)/shard_map/ppermute | solution.py:20
  233.3 5.3 %collective-permute-done.70 = f32[8,64]{1,0:T(8,128)S(1)} collective-permute-done((f32[8,64]{1,0:T(8,128)S(1)}, f32[8,64]{1,0:T(8,128)S(1)}, u32[]{:S(2)}, u32[]{:S(2)}) %collective-permute-start.70) | collective-permute-done | bytes 2080 | tf_op jit(solution)/shard_map/ppermute | solution.py:20
  257.0 4.7 %collective-permute-done.79 = f32[2,24,24]{2,1,0:T(8,128)S(1)} collective-permute-done((f32[2,24,24]{2,1,0:T(8,128)S(1)}, f32[2,24,24]{2,1,0:T(8,128)S(1)}, u32[]{:S(2)}, u32[]{:S(2)}) %collective-permute-start.79) | collective-permute-done | bytes 4640 | tf_op jit(solution)/shard_map/ppermute | solution.py:45
  (299 shorter events, 131.0 us)
Async XLA Ops:
  3.5 11.4 %collective-permute-start.3 = (f32[16,64]{1,0:T(8,128)S(1)}, f32[16,64]{1,0:T(8,128)S(1)}, u32[]{:S(2)}, u32[]{:S(2)}) collective-permute-start(f32[16,64]{1,0:T(8,128)S(1)} %get-tuple-element.35), channel_id=1, source_target_pairs={{0,28},{1,29},{2,30},{3,31},{4,0},{5,1},{6,2},{7,3},{8,4},{9,5},{1... | collective-permute-start | bytes 12296 | tf_op jit(solution)/shard_map/ppermute | solution.py:20
  30.5 11.5 %collective-permute-start.9 = (f32[17,128]{1,0:T(8,128)S(1)}, f32[17,128]{1,0:T(8,128)S(1)}, u32[]{:S(2)}, u32[]{:S(2)}) collective-permute-start(f32[17,128]{1,0:T(8,128)S(1)} %concatenate.201), channel_id=1, source_target_pairs={{0,16},{1,17},{2,18},{3,19},{4,20},{5,21},{6,22},{7,23},{8,24},{9,... | collective-permute-start | bytes 26120 | tf_op jit(solution)/shard_map/ppermute | solution.py:20
  30.6 10.1 %collective-permute-start.8 = (f32[17,64]{1,0:T(8,128)S(1)}, f32[17,64]{1,0:T(8,128)S(1)}, u32[]{:S(2)}, u32[]{:S(2)}) collective-permute-start(f32[17,64]{1,0:T(8,128)S(1)} %get-tuple-element.17), channel_id=1, source_target_pairs={{0,4},{1,5},{2,6},{3,7},{4,8},{5,9},{6,10},{7,11},{8,12},{9,13},{1... | collective-permute-start | bytes 13064 | tf_op jit(solution)/shard_map/ppermute | solution.py:20
  78.2 11.5 %collective-permute-start.24 = (f32[8,128]{1,0:T(8,128)S(1)}, f32[8,128]{1,0:T(8,128)S(1)}, u32[]{:S(2)}, u32[]{:S(2)}) collective-permute-start(f32[8,128]{1,0:T(8,128)S(1)} %concatenate.203), channel_id=1, source_target_pairs={{0,16},{1,17},{2,18},{3,19},{4,20},{5,21},{6,22},{7,23},{8,24},{9,... | collective-permute-start | bytes 12296 | tf_op jit(solution)/shard_map/ppermute | solution.py:20
  78.2 10.2 %collective-permute-start.23 = (f32[8,64]{1,0:T(8,128)S(1)}, f32[8,64]{1,0:T(8,128)S(1)}, u32[]{:S(2)}, u32[]{:S(2)}) collective-permute-start(f32[8,64]{1,0:T(8,128)S(1)} %get-tuple-element.29), channel_id=1, source_target_pairs={{0,4},{1,5},{2,6},{3,7},{4,8},{5,9},{6,10},{7,11},{8,12},{9,13},{1... | collective-permute-start | bytes 6152 | tf_op jit(solution)/shard_map/ppermute | solution.py:20
  78.3 10.2 %collective-permute-start.22 = (f32[8,64]{1,0:T(8,128)S(1)}, f32[8,64]{1,0:T(8,128)S(1)}, u32[]{:S(2)}, u32[]{:S(2)}) collective-permute-start(f32[8,64]{1,0:T(8,128)S(1)} %get-tuple-element.30), channel_id=1, source_target_pairs={{0,28},{1,29},{2,30},{3,31},{4,0},{5,1},{6,2},{7,3},{8,4},{9,5},{1... | collective-permute-start | bytes 6152 | tf_op jit(solution)/shard_map/ppermute | solution.py:20
  90.6 10.2 %collective-permute-start.28 = (f32[8,64]{1,0:T(8,128)S(1)}, f32[8,64]{1,0:T(8,128)S(1)}, u32[]{:S(2)}, u32[]{:S(2)}) collective-permute-start(f32[8,64]{1,0:T(8,128)S(1)} %get-tuple-element.64), channel_id=1, source_target_pairs={{0,28},{1,29},{2,30},{3,31},{4,0},{5,1},{6,2},{7,3},{8,4},{9,5},{1... | collective-permute-start | bytes 6152 | tf_op jit(solution)/shard_map/ppermute | solution.py:20
  90.6 10.2 %collective-permute-start.27 = (f32[8,64]{1,0:T(8,128)S(1)}, f32[8,64]{1,0:T(8,128)S(1)}, u32[]{:S(2)}, u32[]{:S(2)}) collective-permute-start(f32[8,64]{1,0:T(8,128)S(1)} %get-tuple-element.65), channel_id=1, source_target_pairs={{0,4},{1,5},{2,6},{3,7},{4,8},{5,9},{6,10},{7,11},{8,12},{9,13},{1... | collective-permute-start | bytes 6152 | tf_op jit(solution)/shard_map/ppermute | solution.py:20
  112.7 20.3 %collective-permute-start.34 = (f32[8,128]{1,0:T(8,128)S(1)}, f32[8,128]{1,0:T(8,128)S(1)}, u32[]{:S(2)}, u32[]{:S(2)}) collective-permute-start(f32[8,128]{1,0:T(8,128)S(1)} %concatenate.205), channel_id=1, source_target_pairs={{0,16},{1,17},{2,18},{3,19},{4,20},{5,21},{6,22},{7,23},{8,24},{9,... | collective-permute-start | bytes 12296 | tf_op jit(solution)/shard_map/ppermute | solution.py:20
  112.7 10.2 %collective-permute-start.33 = (f32[8,64]{1,0:T(8,128)S(1)}, f32[8,64]{1,0:T(8,128)S(1)}, u32[]{:S(2)}, u32[]{:S(2)}) collective-permute-start(f32[8,64]{1,0:T(8,128)S(1)} %get-tuple-element.25), channel_id=1, source_target_pairs={{0,4},{1,5},{2,6},{3,7},{4,8},{5,9},{6,10},{7,11},{8,12},{9,13},{1... | collective-permute-start | bytes 6152 | tf_op jit(solution)/shard_map/ppermute | solution.py:20
  112.8 10.1 %collective-permute-start.32 = (f32[8,64]{1,0:T(8,128)S(1)}, f32[8,64]{1,0:T(8,128)S(1)}, u32[]{:S(2)}, u32[]{:S(2)}) collective-permute-start(f32[8,64]{1,0:T(8,128)S(1)} %get-tuple-element.26), channel_id=1, source_target_pairs={{0,28},{1,29},{2,30},{3,31},{4,0},{5,1},{6,2},{7,3},{8,4},{9,5},{1... | collective-permute-start | bytes 6152 | tf_op jit(solution)/shard_map/ppermute | solution.py:20
  117.5 10.2 %collective-permute-start.31 = (f32[8,64]{1,0:T(8,128)S(1)}, f32[8,64]{1,0:T(8,128)S(1)}, u32[]{:S(2)}, u32[]{:S(2)}) collective-permute-start(f32[8,64]{1,0:T(8,128)S(1)} %get-tuple-element.27), channel_id=1, source_target_pairs={{0,1},{1,2},{2,3},{3,4},{4,5},{5,6},{6,7},{7,8},{8,9},{9,10},{10,1... | collective-permute-start | bytes 6152 | tf_op jit(solution)/shard_map/ppermute | solution.py:20
  117.5 10.2 %collective-permute-start.30 = (f32[8,64]{1,0:T(8,128)S(1)}, f32[8,64]{1,0:T(8,128)S(1)}, u32[]{:S(2)}, u32[]{:S(2)}) collective-permute-start(f32[8,64]{1,0:T(8,128)S(1)} %get-tuple-element.28), channel_id=1, source_target_pairs={{0,31},{1,0},{2,1},{3,2},{4,3},{5,4},{6,5},{7,6},{8,7},{9,8},{10,9... | collective-permute-start | bytes 6152 | tf_op jit(solution)/shard_map/ppermute | solution.py:20
  122.9 11.0 %collective-permute-start.53 = (f32[1,32]{1,0:T(1,128)S(1)}, f32[1,32]{1,0:T(1,128)S(1)}, u32[]{:S(2)}, u32[]{:S(2)}) collective-permute-start(f32[1,32]{1,0:T(1,128)S(1)} %get-tuple-element.82), channel_id=1, source_target_pairs={{0,4},{1,5},{2,6},{3,7},{4,8},{5,9},{6,10},{7,11},{8,12},{9,13},{1... | collective-permute-start | bytes 392 | tf_op jit(solution)/shard_map/ppermute | solution.py:20
  123.0 11.0 %collective-permute-start.52 = (f32[1,32]{1,0:T(1,128)S(1)}, f32[1,32]{1,0:T(1,128)S(1)}, u32[]{:S(2)}, u32[]{:S(2)}) collective-permute-start(f32[1,32]{1,0:T(1,128)S(1)} %get-tuple-element.83), channel_id=1, source_target_pairs={{0,28},{1,29},{2,30},{3,31},{4,0},{5,1},{6,2},{7,3},{8,4},{9,5},{1... | collective-permute-start | bytes 392 | tf_op jit(solution)/shard_map/ppermute | solution.py:20
  127.7 10.5 %collective-permute-start.50 = (f32[1,32]{1,0:T(1,128)S(1)}, f32[1,32]{1,0:T(1,128)S(1)}, u32[]{:S(2)}, u32[]{:S(2)}) collective-permute-start(f32[1,32]{1,0:T(1,128)S(1)} %get-tuple-element.85), channel_id=1, source_target_pairs={{0,31},{1,0},{2,1},{3,2},{4,3},{5,4},{6,5},{7,6},{8,7},{9,8},{10,9... | collective-permute-start | bytes 392 | tf_op jit(solution)/shard_map/ppermute | solution.py:20
  150.9 11.5 %collective-permute-start.44 = (f32[8,128]{1,0:T(8,128)S(1)}, f32[8,128]{1,0:T(8,128)S(1)}, u32[]{:S(2)}, u32[]{:S(2)}) collective-permute-start(f32[8,128]{1,0:T(8,128)S(1)} %concatenate.207), channel_id=1, source_target_pairs={{0,16},{1,17},{2,18},{3,19},{4,20},{5,21},{6,22},{7,23},{8,24},{9,... | collective-permute-start | bytes 12296 | tf_op jit(solution)/shard_map/ppermute | solution.py:20
  150.9 10.3 %collective-permute-start.43 = (f32[8,64]{1,0:T(8,128)S(1)}, f32[8,64]{1,0:T(8,128)S(1)}, u32[]{:S(2)}, u32[]{:S(2)}) collective-permute-start(f32[8,64]{1,0:T(8,128)S(1)} %get-tuple-element.21), channel_id=1, source_target_pairs={{0,4},{1,5},{2,6},{3,7},{4,8},{5,9},{6,10},{7,11},{8,12},{9,13},{1... | collective-permute-start | bytes 6152 | tf_op jit(solution)/shard_map/ppermute | solution.py:20
  151.0 10.3 %collective-permute-start.42 = (f32[8,64]{1,0:T(8,128)S(1)}, f32[8,64]{1,0:T(8,128)S(1)}, u32[]{:S(2)}, u32[]{:S(2)}) collective-permute-start(f32[8,64]{1,0:T(8,128)S(1)} %get-tuple-element.22), channel_id=1, source_target_pairs={{0,28},{1,29},{2,30},{3,31},{4,0},{5,1},{6,2},{7,3},{8,4},{9,5},{1... | collective-permute-start | bytes 6152 | tf_op jit(solution)/shard_map/ppermute | solution.py:20
  163.7 11.5 %collective-permute-start.49 = (f32[8,64]{1,0:T(8,128)S(1)}, f32[8,64]{1,0:T(8,128)S(1)}, u32[]{:S(2)}, u32[]{:S(2)}) collective-permute-start(f32[8,64]{1,0:T(8,128)S(1)} %concatenate.208), channel_id=1, source_target_pairs={{0,16},{1,17},{2,18},{3,19},{4,20},{5,21},{6,22},{7,23},{8,24},{9,... | collective-permute-start | bytes 6152 | tf_op jit(solution)/shard_map/ppermute | solution.py:20
  163.7 10.1 %collective-permute-start.48 = (f32[8,32]{1,0:T(8,128)S(1)}, f32[8,32]{1,0:T(8,128)S(1)}, u32[]{:S(2)}, u32[]{:S(2)}) collective-permute-start(f32[8,32]{1,0:T(8,128)S(1)} %get-tuple-element.43), channel_id=1, source_target_pairs={{0,4},{1,5},{2,6},{3,7},{4,8},{5,9},{6,10},{7,11},{8,12},{9,13},{1... | collective-permute-start | bytes 3080 | tf_op jit(solution)/shard_map/ppermute | solution.py:20
  194.8 11.5 %collective-permute-start.64 = (f32[8,64]{1,0:T(8,128)S(1)}, f32[8,64]{1,0:T(8,128)S(1)}, u32[]{:S(2)}, u32[]{:S(2)}) collective-permute-start(f32[8,64]{1,0:T(8,128)S(1)} %concatenate.211), channel_id=1, source_target_pairs={{0,16},{1,17},{2,18},{3,19},{4,20},{5,21},{6,22},{7,23},{8,24},{9,... | collective-permute-start | bytes 6152 | tf_op jit(solution)/shard_map/ppermute | solution.py:20
  194.8 10.6 %collective-permute-start.63 = (f32[8,32]{1,0:T(8,128)S(1)}, f32[8,32]{1,0:T(8,128)S(1)}, u32[]{:S(2)}, u32[]{:S(2)}) collective-permute-start(f32[8,32]{1,0:T(8,128)S(1)} %get-tuple-element.39), channel_id=1, source_target_pairs={{0,4},{1,5},{2,6},{3,7},{4,8},{5,9},{6,10},{7,11},{8,12},{9,13},{1... | collective-permute-start | bytes 3080 | tf_op jit(solution)/shard_map/ppermute | solution.py:20
  194.9 10.6 %collective-permute-start.62 = (f32[8,32]{1,0:T(8,128)S(1)}, f32[8,32]{1,0:T(8,128)S(1)}, u32[]{:S(2)}, u32[]{:S(2)}) collective-permute-start(f32[8,32]{1,0:T(8,128)S(1)} %get-tuple-element.40), channel_id=1, source_target_pairs={{0,28},{1,29},{2,30},{3,31},{4,0},{5,1},{6,2},{7,3},{8,4},{9,5},{1... | collective-permute-start | bytes 3080 | tf_op jit(solution)/shard_map/ppermute | solution.py:20
  (65 other events, 429.7 us)
